TPU v7x, 512 devices: a whole 4x8x8 slice. The times are simulated.
512 devices in a mesh: rep: 8 (over y_hi, core), tp: 64 (over x, z, y_lo).
Axes of the slice: x: 4, y: 8 (y_hi: 4, y_lo: 2; y = y_hi * 2 + y_lo), z: 8, core: 2. Of those that a mesh axis runs over, the one named last changes fastest.
Arguments:
- tokens: bfloat16 [4096, 6144], P(('rep', 'tp')), parts along dimension 0, may hold values from -6 to 6
- ln_gain: bfloat16 [6144], replicated, may hold values from 0.5 to 1.5
- ln_bias: bfloat16 [6144], replicated, may hold values from -4 to 4
- w_qkv: bfloat16 [6144, 18432], P(None, 'tp'), may hold values from -0.078125 to 0.078125
- b_qkv: bfloat16 [18432], P('tp'), may hold values from -6 to 6
- w_dense: bfloat16 [6144, 6144], P(None, 'tp'), may hold values from -0.625 to 0.625
- b_dense: bfloat16 [6144], replicated, may hold values from -6 to 6
- prefix_kv: bfloat16 [2, 32, 128, 6144], P(None, 'rep', None, 'tp'), parts along dimension 1, may hold values from -110 to 110
- decode_kv: bfloat16 [2, 256, 16, 6144], P(None, 'rep', None, 'tp'), parts along dimension 1, may hold values from -110 to 110
- prefix_lens: int32 [32], P('rep'), parts along dimension 0, may hold values from 0 to 128, as said below
- span_request: int32 [32], P('rep'), parts along dimension 0, may hold values from 0 to 3, each once
- decode_lens: int32 [256], P('rep'), parts along dimension 0, may hold values from 1 to 16, 256 in all
- slot_valid: int32 [256, 16], P('rep'), parts along dimension 0, may hold values 0 or 1
Outputs:
- layer_out: bfloat16 [4096, 6144], P(('rep', 'tp')), parts along dimension 0
There are 8 independent parts, one for each index of `rep`. A program takes and returns all parts, laid end to end along the dimension named above; an argument that names none is the same for every part. Nothing has to cross between parts.
Inputs may be any that keep to these rules, and one draw needn't show every extreme that they name: `prefix_lens`: some request slot has exactly 128 cached tokens. `span_request`: each request slot is continued by exactly one span. `decode_lens`: the lengths sum to 256 and one equals 16.
All inputs are finite; a program needn't handle non-finite values.
Results may differ from a plain program's by a relative error of at most 0.012.
The roundings to bfloat16 on the way count: a program that leaves them out, or rounds other values in their place, can miss the bound.
Values may be sent and summed in bfloat16 or wider, within the bound.
No kernel may reach another device: no remote copies, remote signals or barrier semaphores. Data moves between devices by JAX's collectives and lax.ppermute only.
A program may use at most 64 MiB of HBM per device.

v0:
```python
import math

import jax
import jax.numpy as jnp
from jax import lax
from jax.sharding import PartitionSpec as P

ROT = 24


def layer_norm(rows, gain, shift):
    value_matrix = rows.astype(jnp.float32)
    center = value_matrix - jnp.mean(value_matrix, axis=-1, keepdims=True)
    spread = jnp.mean(center * center, axis=-1, keepdims=True)
    scaled = center * lax.rsqrt(spread + 1e-05)
    return (scaled * gain.astype(jnp.float32) + shift.astype(jnp.float32)).astype(jnp.bfloat16)


def rotary_tables(places, rot_dims):
    counter = jnp.arange(rot_dims // 2, dtype=jnp.float32)
    inverse = jnp.exp(counter * (-2.0 * math.log(10000.0) / rot_dims))
    angles = places.astype(jnp.float32)[:, None] * inverse[None, :]
    return (jnp.cos(angles), jnp.sin(angles))


def rotate(field, cosine, sine):
    half = cosine.shape[-1]
    first = field[..., :half]
    second = field[..., half : 2 * half]
    return jnp.concatenate(
        [first * cosine - second * sine, second * cosine + first * sine, field[..., 2 * half :]],
        axis=-1,
    )


def token_places(span_lens, cache_lens, span_rows):
    within = jnp.arange(span_rows, dtype=jnp.int32)
    prefill = (span_lens[:, None] + within[None, :]).reshape(-1)
    return jnp.concatenate([prefill, cache_lens])


def batch_stacked(form, left, right):
    return jnp.einsum(form, left, right, preferred_element_type=jnp.float32)


def attend(logit_scores, live, value_matrix):
    peaks = jnp.max(jnp.where(live, logit_scores, -1e30), axis=-1, keepdims=True)
    raised = jnp.where(live, jnp.exp(logit_scores - peaks), 0.0)
    softmax_weights = (raised / jnp.sum(raised, axis=-1, keepdims=True)).astype(jnp.bfloat16)
    return batch_stacked("lsw,lwe->lse", softmax_weights, value_matrix).astype(jnp.bfloat16)


def prefill_attention(
    query, keys, value_matrix, prefix_keys, prefix_vals, span_lens, decode_rows, score_scale
):
    spans = prefix_keys.shape[0]
    slots = prefix_keys.shape[1]
    span_rows = (query.shape[0] - decode_rows) // spans
    prefill_rows = spans * span_rows
    head = query.shape[-1]
    prefill_query_span = query[:prefill_rows].reshape(spans, span_rows, head)
    combined_key_rows = jnp.concatenate(
        [prefix_keys, keys[:prefill_rows].reshape(spans, span_rows, head)], axis=1
    )
    all_vals = jnp.concatenate(
        [prefix_vals, value_matrix[:prefill_rows].reshape(spans, span_rows, head)], axis=1
    )
    logit_scores = (
        batch_stacked("jrf,jyf->jry", prefill_query_span, combined_key_rows) * score_scale
    )
    column = jnp.arange(slots + span_rows, dtype=jnp.int32)[None, None, :]
    row_index = jnp.arange(span_rows, dtype=jnp.int32)[None, :, None]
    live = jnp.where(column < slots, column < span_lens[:, None, None], column - slots <= row_index)
    return attend(logit_scores, live, all_vals).reshape(prefill_rows, head)


def decode_attention(
    query, keys, value_matrix, stored_key_cache, cache_vals, cache_lens, slot_valid, score_scale
):
    decode_rows = stored_key_cache.shape[0]
    slots = stored_key_cache.shape[1]
    first_row = query.shape[0] - decode_rows
    decode_query_row = query[first_row:]
    own_keys = keys[first_row:]
    own_vals = value_matrix[first_row:]
    cache_present = (
        batch_stacked("jrf,jyf->jry", decode_query_row[:, None, :], stored_key_cache) * score_scale
    )
    itself = (
        jnp.sum(decode_query_row.astype(jnp.float32) * own_keys.astype(jnp.float32), axis=-1)[
            :, None, None
        ]
        * score_scale
    )
    logit_scores = jnp.concatenate([cache_present, itself], axis=-1)
    column = jnp.arange(slots, dtype=jnp.int32)[None, :]
    live_cache = (column < cache_lens[:, None]) & (slot_valid == 1)
    live = jnp.concatenate([live_cache, jnp.ones((decode_rows, 1), dtype=bool)], axis=-1)[
        :, None, :
    ]
    all_vals = jnp.concatenate([cache_vals, own_vals[:, None, :]], axis=1)
    return attend(logit_scores, live, all_vals)[:, 0, :]


def on_device(
    tokens,
    ln_gain,
    ln_bias,
    w_qkv,
    b_qkv,
    w_dense,
    b_dense,
    prefix_kv,
    decode_kv,
    prefix_lens,
    span_request,
    decode_lens,
    slot_valid,
):
    normed = layer_norm(tokens, ln_gain, ln_bias)
    joined = jnp.dot(
        lax.all_gather(normed, "tp", axis=0, tiled=True), w_qkv, preferred_element_type=jnp.float32
    )
    joined = joined + b_qkv.astype(jnp.float32)
    head = joined.shape[1] // 3
    token_count = joined.shape[0]
    spans = prefix_kv.shape[1]
    decode_rows = decode_kv.shape[1]
    span_rows = (token_count - decode_rows) // spans
    span_lens = jnp.take(prefix_lens, span_request, axis=0)
    cosine, sine = rotary_tables(token_places(span_lens, decode_lens, span_rows), ROT)
    query = rotate(joined[:, :head], cosine, sine).astype(jnp.bfloat16)
    keys = rotate(joined[:, head : 2 * head], cosine, sine).astype(jnp.bfloat16)
    value_matrix = joined[:, 2 * head :].astype(jnp.bfloat16)
    prefix_keys = jnp.take(prefix_kv[0], span_request, axis=0)
    prefix_vals = jnp.take(prefix_kv[1], span_request, axis=0)
    score_scale = 1.0 / math.sqrt(head)
    early = prefill_attention(
        query, keys, value_matrix, prefix_keys, prefix_vals, span_lens, decode_rows, score_scale
    )
    late = decode_attention(
        query, keys, value_matrix, decode_kv[0], decode_kv[1], decode_lens, slot_valid, score_scale
    )
    heads_out = jnp.concatenate([early, late], axis=0)
    mixed = jnp.dot(
        lax.all_gather(heads_out, "tp", axis=1, tiled=True),
        w_dense,
        preferred_element_type=jnp.float32,
    )
    own_rows = lax.all_to_all(mixed, "tp", split_axis=0, concat_axis=1, tiled=True)
    attn = (own_rows + b_dense.astype(jnp.float32)).astype(jnp.bfloat16)
    return (attn.astype(jnp.float32) + tokens.astype(jnp.float32)).astype(jnp.bfloat16)


def solution(mesh):
    placed = (
        P(("rep", "tp"), None),
        P(),
        P(),
        P(None, "tp"),
        P("tp"),
        P(None, "tp"),
        P(),
        P(None, "rep", None, "tp"),
        P(None, "rep", None, "tp"),
        P("rep"),
        P("rep"),
        P("rep"),
        P("rep", None),
    )
    return jax.shard_map(
        on_device, mesh=mesh, in_specs=placed, out_specs=P(("rep", "tp"), None), check_vma=False
    )
```

profile of v0, /device:TPU:40, one launch (start us, length us, event | category | flops | bytes accessed | tf_op | source)
XLA Modules:
  0.0 730.7 jit_solution(18445028543384354713)
XLA Ops:
  10.5 1.6 fusion.15
  14.1 1.3 gather_fusion
  16.8 1.6 slice_bitcast_fusion.1
  18.5 2.1 gather_fusion.2
  20.5 2.1 gather_fusion.1
  24.5 1.3 iota_compare_fusion.2
  25.8 1.3 fusion.44
  27.7 1.6 slice_bitcast_fusion
  29.3 1.7 broadcast_select_fusion
  31.0 304.9 %all-gather.3.cloned.1.call-done = bf16[512,6144]{1,0:T(8,128)(2,1)} async-done(((bf16[8,6144]{1,0:T(8,128)(2,1)}), bf16[512,6144]{1,0:T(8,128)(2,1)}) %all-gather.3.cloned.1.call-update) | async-done | bytes 6291472 | tf_op jit(solution)/shard_map/all_gather | solution.py:122
  335.9 4.8 fusion.55
  343.7 1.4 copy.29
  345.7 1.5 copy.43
  351.0 1.3 fusion.46
  353.1 1.7 multiply_reduce_fusion
  354.8 1.4 copy.40
  356.2 1.6 reshape.178
  357.8 1.5 copy.25
  359.4 1.6 reshape.177
  361.0 1.6 reshape.179
  362.6 1.5 copy.27
  367.3 2.9 convolution_convert_fusion
  370.2 1.6 copy.28
  371.8 1.7 reshape.180
  373.5 1.6 pad_maximum_fusion.2
  375.1 318.0 %all-gather.5.cloned.1.call-done = bf16[512,6144]{0,1:T(8,128)(2,1)} async-done(((bf16[512,96]{0,1:T(8,128)(2,1)}), bf16[512,6144]{0,1:T(8,128)(2,1)}) %all-gather.5.cloned.1.call-update) | async-done | bytes 6291472 | tf_op jit(solution)/shard_map/all_gather | solution.py:146
  693.1 5.6 convolution_bitcast_fusion
  698.7 8.9 %all-to-all-start = ((f32[64,8,96]{2,1,0:T(8,128)}), f32[64,8,96]{2,1,0:T(8,128)}, u32[]{:S(2)}, u32[]{:S(2)}) async-start(f32[64,8,96]{2,1,0:T(8,128)} %convolution_bitcast_fusion), calls=%async_computation | async-start | bytes 524288 | tf_op jit(solution)/shard_map/all_to_all | solution.py:150
  708.2 10.4 %all-to-all-done = f32[64,8,96]{2,1,0:T(8,128)} async-done(((f32[64,8,96]{2,1,0:T(8,128)}), f32[64,8,96]{2,1,0:T(8,128)}, u32[]{:S(2)}, u32[]{:S(2)}) %all-to-all-start) | async-done | bytes 196640 | tf_op jit(solution)/shard_map/all_to_all | solution.py:150
  718.7 1.7 copy.31
  720.4 1.8 all_to_all.17
  722.2 1.7 fusion.16
  (47 shorter events, 21.7 us)
Async XLA Ops:
  6.5 329.4 %copy-start = (bf16[6144,288]{0,1:T(8,128)(2,1)S(1)}, bf16[6144,288]{0,1:T(8,128)(2,1)}, u32[]{:S(2)}) copy-start(bf16[6144,288]{0,1:T(8,128)(2,1)} %param.18) | copy-start | bytes 10616836
  6.5 329.4 %all-gather.3.cloned.1.call-start = ((), (), s32[]{:S(2)}) async-start(), calls=%async_computation.1 | async-start | bytes 6389760 | tf_op jit(solution)/shard_map/all_gather | solution.py:122
  12.2 680.9 %all-gather.5.cloned.1.call-start = ((), (), s32[]{:S(2)}) async-start(), calls=%async_computation.2 | async-start | bytes 6389760 | tf_op jit(solution)/shard_map/all_gather | solution.py:146
  16.1 0.6 copy-start.3
  31.0 310.5 %copy-start.4 = (f32[12]{0:T(128)S(1)}, f32[12]{0:T(128)}, u32[]{:S(2)}) copy-start(f32[12]{0:T(128)} %multiply_exponential_fusion) | copy-start | bytes 148
  365.4 0.8 copy-start.1
  367.3 340.3 %copy-start.2 = (bf16[6144]{0:T(1024)(128)(2,1)S(1)}, bf16[6144]{0:T(1024)(128)(2,1)}, u32[]{:S(2)}) copy-start(bf16[6144]{0:T(1024)(128)(2,1)} %param.21) | copy-start | bytes 36868
  698.7 20.0 %all-to-all-start = ((f32[64,8,96]{2,1,0:T(8,128)}), f32[64,8,96]{2,1,0:T(8,128)}, u32[]{:S(2)}, u32[]{:S(2)}) async-start(f32[64,8,96]{2,1,0:T(8,128)} %convolution_bitcast_fusion), calls=%async_computation | async-start | bytes 524288 | tf_op jit(solution)/shard_map/all_to_all | solution.py:150
Sparse Core Ops, SparseCore 0:
  12.3 323.5 all-gather.2
  375.2 317.7 all-gather.4
where the time goes:
time: 732 us; the launch traced here: 731 us
  waiting for transfers between devices  633 us (86%)
  local copies, waits for them, and re-layouts  31.8 us (4%)
  other arithmetic  28.4 us (4%)
  matrix products  14.6 us (2%)
  between operations  13.5 us (2%)
  starting transfers between devices  8.97 us (1%)
    all_gather x1, waiting for transfers between devices, on_device(): lax.all_gather(heads_out, 'tp', axis=1, tiled=True)  318 us
    all_gather x1, waiting for transfers between devices, on_device(): lax.all_gather(normed, 'tp', axis=0, tiled=True)  305 us
  transfers between devices with their start and end apart: 3, of which 3 were waited for; matrix products, arithmetic and copies ran while one was open for 3% of the time, Pallas kernels for 0%

commit v1 on v0

--- a/solution.py
+++ b/solution.py
@@ -102,6 +102,20 @@
     return attend(logit_scores, live, all_vals)[:, 0, :]
 
 
+TP = ("x", "z", "yl")
+
+
+def gather_rows(block):
+    pair = lax.all_gather(block, "yl", axis=0, tiled=True)
+    return lax.all_gather(pair, ("x", "z"), axis=0, tiled=True)
+
+
+def gather_heads(block):
+    pair = lax.all_gather(block, "yl", axis=0, tiled=False)
+    every = lax.all_gather(pair, ("x", "z"), axis=0, tiled=False)
+    return every.reshape((-1,) + block.shape)
+
+
 def on_device(
     tokens,
     ln_gain,
@@ -118,9 +132,7 @@
     slot_valid,
 ):
     normed = layer_norm(tokens, ln_gain, ln_bias)
-    joined = jnp.dot(
-        lax.all_gather(normed, "tp", axis=0, tiled=True), w_qkv, preferred_element_type=jnp.float32
-    )
+    joined = jnp.dot(gather_rows(normed), w_qkv, preferred_element_type=jnp.float32)
     joined = joined + b_qkv.astype(jnp.float32)
     head = joined.shape[1] // 3
     token_count = joined.shape[0]
@@ -142,32 +154,46 @@
         query, keys, value_matrix, decode_kv[0], decode_kv[1], decode_lens, slot_valid, score_scale
     )
     heads_out = jnp.concatenate([early, late], axis=0)
-    mixed = jnp.dot(
-        lax.all_gather(heads_out, "tp", axis=1, tiled=True),
-        w_dense,
+    every_head = gather_heads(heads_out)
+    heads = every_head.shape[0]
+    mixed = lax.dot_general(
+        every_head,
+        w_dense.reshape(heads, head, w_dense.shape[1]),
+        (((0, 2), (0, 1)), ((), ())),
         preferred_element_type=jnp.float32,
     )
-    own_rows = lax.all_to_all(mixed, "tp", split_axis=0, concat_axis=1, tiled=True)
-    attn = (own_rows + b_dense.astype(jnp.float32)).astype(jnp.bfloat16)
-    return (attn.astype(jnp.float32) + tokens.astype(jnp.float32)).astype(jnp.bfloat16)
+    attn = (mixed + b_dense_own(b_dense, mixed.shape[1])).astype(jnp.bfloat16)
+    own_rows = lax.all_to_all(attn, TP, split_axis=0, concat_axis=1, tiled=True)
+    return (own_rows.astype(jnp.float32) + tokens.astype(jnp.float32)).astype(jnp.bfloat16)
+
+
+def b_dense_own(b_dense, width):
+    start = lax.axis_index(TP) * width
+    return lax.dynamic_slice_in_dim(b_dense, start, width).astype(jnp.float32)
 
 
 def solution(mesh):
+    reps = mesh.shape["rep"]
+    coords = [d.coords for d in mesh.devices[0]]
+    x_size = len({c[0] for c in coords})
+    z_size = len({c[2] for c in coords})
+    devices = mesh.devices.reshape(reps, x_size, z_size, -1)
+    mesh = jax.sharding.Mesh(devices, ("rep",) + TP)
     placed = (
-        P(("rep", "tp"), None),
+        P(("rep",) + TP, None),
         P(),
         P(),
-        P(None, "tp"),
-        P("tp"),
-        P(None, "tp"),
+        P(None, TP),
+        P(TP),
+        P(None, TP),
         P(),
-        P(None, "rep", None, "tp"),
-        P(None, "rep", None, "tp"),
+        P(None, "rep", None, TP),
+        P(None, "rep", None, TP),
         P("rep"),
         P("rep"),
         P("rep"),
         P("rep", None),
     )
     return jax.shard_map(
-        on_device, mesh=mesh, in_specs=placed, out_specs=P(("rep", "tp"), None), check_vma=False
+        on_device, mesh=mesh, in_specs=placed, out_specs=P(("rep",) + TP, None), check_vma=False
     )

time: 732 us -> 289 us (0.39)
  the two profiles are of different devices: /device:TPU:40 before, /device:TPU:8 now
where the time goes in v1:
time: 289 us; the launch traced here: 287 us
  waiting for transfers between devices  163 us (56%)
  local copies, waits for them, and re-layouts  37.1 us (13%)
  blocking collectives  31.7 us (11%)
  other arithmetic  27 us (9%)
  matrix products  15.2 us (5%)
  between operations  13.5 us (5%)
    all_gather x1, waiting for transfers between devices, gather_heads(): every = lax.all_gather(pair, ('x', 'z'), axis=0, tiled=False)  86.4 us
    all_gather x1, waiting for transfers between devices, gather_rows(): return lax.all_gather(pair, ('x', 'z'), axis=0, tiled=True)  76.4 us
    all_to_all x1, blocking collectives, on_device(): own_rows = lax.all_to_all(attn, TP, split_axis=0, concat_axis=1, tiled=True)  17.3 us
    all_gather x1, blocking collectives, gather_rows(): pair = lax.all_gather(block, 'yl', axis=0, tiled=True)  9.15 us
    dot_general x1, matrix products, on_device(): lax.dot_general(every_head, w_dense.reshape(heads, head, w_dense.shape[1]...  6.27 us
  transfers between devices with their start and end apart: 2, of which 2 were waited for; matrix products, arithmetic and copies ran while one was open for 8% of the time, Pallas kernels for 0%

profile of v1, /device:TPU:8, one launch (start us, length us, event | category | flops | bytes accessed | tf_op | source)
XLA Modules:
  0.0 287.4 jit_solution(10174321669541422756)
XLA Ops:
  11.3 9.1 %all_gather.18 = bf16[16,6144]{1,0:T(8,128)(2,1)} all-gather(bf16[8,6144]{1,0:T(8,128)(2,1)S(1)} %fusion.26), channel_id=1, replica_groups=mesh['rep'=8,'x'=4,'z'=8,'yl'=2] {'yl'}, dimensions={0}, use_global_device_ids=true | all-gather | bytes 294912 | tf_op jit(solution)/shard_map/all_gather | solution.py:109
  22.5 1.3 gather_fusion
  25.2 1.6 slice_bitcast_fusion.1
  26.8 2.1 gather_fusion.2
  28.9 2.1 gather_fusion.1
  32.8 1.3 iota_compare_fusion.2
  34.1 1.3 fusion.55
  36.0 1.6 slice_bitcast_fusion
  37.6 1.7 broadcast_select_fusion
  39.3 76.4 %all-gather.5.cloned.1.call-done = bf16[512,6144]{1,0:T(8,128)(2,1)} async-done(((bf16[16,6144]{1,0:T(8,128)(2,1)}), bf16[512,6144]{1,0:T(8,128)(2,1)}) %all-gather.5.cloned.1.call-update) | async-done | bytes 6291472 | tf_op jit(solution)/shard_map/all_gather | solution.py:110
  115.7 4.8 %fusion.66 = (bf16[512,288]{0,1:T(8,128)(2,1)S(1)}, f32[512,288]{0,1:T(8,128)S(1)}) fusion(f32[288]{0:T(512)} %convert_element_type.68, bf16[512,6144]{1,0:T(8,128)(2,1)} %all-gather.5.cloned.1.call-done, bf16[6144,288]{0,1:T(8,128)(2,1)S(1)} %copy-done), kind=kOutput, calls=%fused_computation.104 | convolution fusion | flops 1812234240 | bytes 10716288 | tf_op jit(solution)/shard_map/dot_general | solution.py:135
  123.5 1.4 copy.41
  124.9 1.6 reshape.187
  126.6 1.5 copy.39
  128.1 1.6 reshape.185
  129.7 1.6 reshape.186
  131.4 1.5 copy.37
  133.4 1.5 copy.56
  138.7 1.3 fusion.57
  140.8 1.7 multiply_reduce_fusion
  142.5 1.4 copy.54
  147.1 2.9 %convolution_convert_fusion = bf16[4,120,96]{1,2,0:T(8,128)(2,1)} fusion(f32[4,120]{1,0:T(4,128)S(1)} %fusion.67, bf16[4,120,96]{1,2,0:T(8,128)(2,1)} %copy.39, bf16[4,128,96]{1,2,0:T(8,128)(2,1)} %get-tuple-element.18, f32[4,120,248]{2,1,0:T(8,128)} %copy-done.1, pred[120,248]{1,0:T(8,128)(4,1)} %iota_compare_fusion, ...), kind=kOutput, calls=%fused_computation.14 | convolution fusion | flops 24116696 | bytes 791704 | tf_op jit(solution)/shard_map/lsw,lwe->lse/dot_general | solution.py:43
  150.0 1.6 copy.40
  151.5 1.7 reshape.188
  154.2 5.3 %all-gather = bf16[1024,96]{0,1:T(8,128)(2,1)S(1)} all-gather(bf16[512,96]{0,1:T(8,128)(2,1)S(1)} %pad_maximum_fusion.2), channel_id=2, replica_groups=mesh['rep'=8,'x'=4,'z'=8,'yl'=2] {'yl'}, dimensions={0}, use_global_device_ids=true | all-gather | bytes 294912 | tf_op jit(solution)/shard_map/all_gather | solution.py:114
  160.2 3.9 %reshape.190 = bf16[64,96,96]{1,0,2:T(8,128)(2,1)} reshape(bf16[6144,96]{0,1:T(8,128)(2,1)} %param.20) | data formatting | bytes 2359296 | tf_op jit(solution)/shard_map/reshape | solution.py:161
  164.8 86.4 %all-gather.7.cloned.1.call-done = bf16[64,512,96]{1,2,0:T(8,128)(2,1)} async-done(((bf16[2,512,96]{1,2,0:T(8,128)(2,1)}), bf16[64,512,96]{1,2,0:T(8,128)(2,1)}) %all-gather.7.cloned.1.call-update) | async-done | bytes 6291472 | tf_op jit(solution)/shard_map/all_gather | solution.py:115
  251.2 6.3 %fusion.12 = bf16[512,96]{0,1:T(8,128)(2,1)} fusion(bf16[64,512,96]{1,2,0:T(8,128)(2,1)} %all-gather.7.cloned.1.call-done, bf16[64,96,96]{1,0,2:T(8,128)(2,1)} %reshape.190, f32[96]{0:T(128)S(1)} %dynamic-slice_convert_fusion), kind=kOutput, calls=%fused_computation.13 | convolution fusion | flops 604078080 | bytes 7569792 | tf_op jit(solution)/shard_map/dot_general | solution.py:159
  257.4 1.6 copy.44
  259.1 17.3 %all_to_all.13 = bf16[64,8,96]{2,1,0:T(8,128)(2,1)S(1)} all-to-all(bf16[64,8,96]{2,1,0:T(8,128)(2,1)} %bitcast.44), channel_id=1, replica_groups=mesh['rep'=8,'x'=4,'z'=8,'yl'=2] {'x','z','yl'}, dimensions={0} | all-to-all | bytes 196608 | tf_op jit(solution)/shard_map/all_to_all | solution.py:166
  277.2 1.8 reshape.191
  278.9 1.6 fusion.27
  (50 shorter events, 25.0 us)
Async XLA Ops:
  6.5 109.2 %copy-start = (bf16[6144,288]{0,1:T(8,128)(2,1)S(1)}, bf16[6144,288]{0,1:T(8,128)(2,1)}, u32[]{:S(2)}) copy-start(bf16[6144,288]{0,1:T(8,128)(2,1)} %param.18) | copy-start | bytes 10616836
  6.5 109.2 %all-gather.5.cloned.1.call-start = ((), (), s32[]{:S(2)}) async-start(), calls=%async_computation.1 | async-start | bytes 6488064 | tf_op jit(solution)/shard_map/all_gather | solution.py:110
  20.5 230.7 %all-gather.7.cloned.1.call-start = ((), (), s32[]{:S(2)}) async-start(), calls=%async_computation.2 | async-start | bytes 6488064 | tf_op jit(solution)/shard_map/all_gather | solution.py:115
  24.4 0.6 copy-start.2
  39.3 82.6 %copy-start.3 = (f32[12]{0:T(128)S(1)}, f32[12]{0:T(128)}, u32[]{:S(2)}) copy-start(f32[12]{0:T(128)} %multiply_exponential_fusion) | copy-start | bytes 148
  145.2 0.8 copy-start.1
Sparse Core Ops, SparseCore 0:
  20.6 95.0 all-gather.4
  160.3 90.8 all-gather.6

commit v2 on v1

--- a/solution.py
+++ b/solution.py
@@ -154,22 +154,39 @@
         query, keys, value_matrix, decode_kv[0], decode_kv[1], decode_lens, slot_valid, score_scale
     )
     heads_out = jnp.concatenate([early, late], axis=0)
-    every_head = gather_heads(heads_out)
-    heads = every_head.shape[0]
+    attn = dense_in_pairs(heads_out, w_dense, b_dense)
+    return (attn.astype(jnp.float32) + tokens.astype(jnp.float32)).astype(jnp.bfloat16)
+
+
+def dense_in_pairs(heads_out, w_dense, b_dense):
+    partner = [(0, 1), (1, 0)]
+    side = lax.axis_index("yl")
+    rows, head = heads_out.shape
+    width = w_dense.shape[1]
+    groups = lax.axis_index(("x", "z"))
+    per_device = rows // (2 * lax.axis_size(("x", "z")))
+    other_w = lax.ppermute(w_dense, "yl", partner)
+    by_owner = heads_out.reshape(-1, 2, per_device, head)
+    mine = lax.dynamic_index_in_dim(by_owner, side, axis=1, keepdims=False)
+    theirs = lax.dynamic_index_in_dim(by_owner, 1 - side, axis=1, keepdims=False)
+    got = lax.ppermute(theirs, "yl", partner)
+    pair_heads = jnp.stack([mine, got], axis=1)
+    pair_heads = jnp.where(side == 0, pair_heads, pair_heads[:, ::-1])
+    every = lax.all_gather(pair_heads, ("x", "z"), axis=0, tiled=False)
+    pairs = every.shape[0]
+    w_pair = jnp.stack([w_dense, other_w]).reshape(2, pairs, 2, head, width)
     mixed = lax.dot_general(
-        every_head,
-        w_dense.reshape(heads, head, w_dense.shape[1]),
-        (((0, 2), (0, 1)), ((), ())),
+        every,
+        w_pair,
+        (((0, 2, 4), (1, 2, 3)), ((), ())),
         preferred_element_type=jnp.float32,
     )
-    attn = (mixed + b_dense_own(b_dense, mixed.shape[1])).astype(jnp.bfloat16)
-    own_rows = lax.all_to_all(attn, TP, split_axis=0, concat_axis=1, tiled=True)
-    return (own_rows.astype(jnp.float32) + tokens.astype(jnp.float32)).astype(jnp.bfloat16)
-
-
-def b_dense_own(b_dense, width):
-    start = lax.axis_index(TP) * width
-    return lax.dynamic_slice_in_dim(b_dense, start, width).astype(jnp.float32)
+    bias = lax.dynamic_slice_in_dim(b_dense, groups * 2 * width, 2 * width).reshape(2, width)
+    own_first = jnp.stack([bias[side], bias[1 - side]]).astype(jnp.float32)
+    attn = (mixed + own_first).astype(jnp.bfloat16)
+    ordered = jnp.where(side == 0, attn, attn[:, :, ::-1])
+    own_rows = lax.all_to_all(ordered, ("x", "z"), split_axis=0, concat_axis=0, tiled=True)
+    return jnp.transpose(own_rows.reshape(pairs, per_device, 2 * width), (1, 0, 2)).reshape(per_device, -1)
 
 
 def solution(mesh):

time: 289 us -> 286 us (0.990)
  blocking collectives: 31.7 us -> 24.6 us
  waiting for transfers between devices: 163 us -> 157 us
  local copies, waits for them, and re-layouts: 37.1 us -> 42.8 us
  starting transfers between devices: 0.04 us -> 4.92 us
    all_gather x1, waiting for transfers between devices: 86.4 us -> 53.9 us  [dense_in_pairs(): every = lax.all_gather(pair_heads, ('x', 'z'), axis=0, tiled=False)]
    ppermute x0 -> x2, waiting for transfers between devices: none -> 26.4 us  [the longest x1 22.4 us: dense_in_pairs(): other_w = lax.ppermute(w_dense, 'yl', partner)]
    all_gather x1 -> x0, blocking collectives: 5.28 us -> none  [gather_heads(): pair = lax.all_gather(block, 'yl', axis=0, tiled=False)]
    ppermute x0 -> x2, starting transfers between devices: none -> 4.88 us  [the longest x1 2.45 us: dense_in_pairs(): other_w = lax.ppermute(w_dense, 'yl', partner)]
    reshape x1, local copies, waits for them, and re-layouts: 3.86 us -> 0.09 us  [dense_in_pairs(): lax.dynamic_slice_in_dim(b_dense, groups * 2 * width, 2 * width)]
    unnamed x10 -> x11, local copies, waits for them, and re-layouts: 3.62 us -> 6.17 us
  transfers between devices with their start and end apart: 2 -> 4, of which waited for: 2 -> 4; matrix products, arithmetic and copies ran while one was open for 8% -> 8% of each run, Pallas kernels for 0% -> 0%
where the time goes in v2:
time: 286 us; the launch traced here: 285 us
  waiting for transfers between devices  157 us (55%)
  local copies, waits for them, and re-layouts  42.8 us (15%)
  other arithmetic  28.5 us (10%)
  blocking collectives  24.6 us (9%)
  matrix products  13.8 us (5%)
  between operations  13.5 us (5%)
  starting transfers between devices  4.92 us (2%)
    all_gather x1, waiting for transfers between devices, gather_rows(): return lax.all_gather(pair, ('x', 'z'), axis=0, tiled=True)  76.4 us
    all_gather x1, waiting for transfers between devices, dense_in_pairs(): every = lax.all_gather(pair_heads, ('x', 'z'), axis=0, tiled=False)  53.9 us
    ppermute x1, waiting for transfers between devices, dense_in_pairs(): other_w = lax.ppermute(w_dense, 'yl', partner)  22.4 us
    all_to_all x1, blocking collectives, dense_in_pairs(): lax.all_to_all(ordered, ('x', 'z'), split_axis=0, concat_axis=0, tiled=True)  15.4 us
    all_gather x1, blocking collectives, gather_rows(): pair = lax.all_gather(block, 'yl', axis=0, tiled=True)  9.15 us
    unnamed x11, local copies, waits for them, and re-layouts  6.17 us
  transfers between devices with their start and end apart: 4, of which 4 were waited for; matrix products, arithmetic and copies ran while one was open for 8% of the time, Pallas kernels for 0%

profile of v2, /device:TPU:8, one launch (start us, length us, event | category | flops | bytes accessed | tf_op | source)
XLA Modules:
  0.0 284.8 jit_solution(10295921258334912148)
XLA Ops:
  11.3 9.1 %all_gather.12 = bf16[16,6144]{1,0:T(8,128)(2,1)} all-gather(bf16[8,6144]{1,0:T(8,128)(2,1)S(1)} %fusion.28), channel_id=1, replica_groups=mesh['rep'=8,'x'=4,'z'=8,'yl'=2] {'yl'}, dimensions={0}, use_global_device_ids=true | all-gather | bytes 294912 | tf_op jit(solution)/shard_map/all_gather | solution.py:109
  25.2 1.6 slice_bitcast_fusion.1
  26.8 2.1 gather_fusion.2
  28.9 2.1 gather_fusion.1
  36.0 1.6 slice_bitcast_fusion
  37.6 1.7 broadcast_select_fusion
  39.3 76.4 %all-gather.4.cloned.1.call-done = bf16[512,6144]{1,0:T(8,128)(2,1)} async-done(((bf16[16,6144]{1,0:T(8,128)(2,1)}), bf16[512,6144]{1,0:T(8,128)(2,1)}) %all-gather.4.cloned.1.call-update) | async-done | bytes 6291472 | tf_op jit(solution)/shard_map/all_gather | solution.py:110
  115.7 4.8 %fusion.69 = (bf16[512,288]{0,1:T(8,128)(2,1)S(1)}, f32[512,288]{0,1:T(8,128)S(1)}) fusion(f32[288]{0:T(512)} %convert_element_type.75, bf16[512,6144]{1,0:T(8,128)(2,1)} %all-gather.4.cloned.1.call-done, bf16[6144,288]{0,1:T(8,128)(2,1)S(1)} %copy-done), kind=kOutput, calls=%fused_computation.113 | convolution fusion | flops 1812234240 | bytes 10716288 | tf_op jit(solution)/shard_map/dot_general | solution.py:135
  124.9 1.6 reshape.207
  126.6 1.5 copy.44
  128.1 1.6 reshape.205
  129.7 1.6 reshape.206
  131.4 1.5 copy.42
  140.8 1.7 multiply_reduce_fusion
  147.1 2.9 %convolution_convert_fusion = bf16[4,120,96]{1,2,0:T(8,128)(2,1)} fusion(f32[4,120]{1,0:T(4,128)S(1)} %fusion.70, bf16[4,120,96]{1,2,0:T(8,128)(2,1)} %copy.44, bf16[4,128,96]{1,2,0:T(8,128)(2,1)} %get-tuple-element.22, f32[4,120,248]{2,1,0:T(8,128)} %copy-done.1, pred[120,248]{1,0:T(8,128)(4,1)} %iota_compare_fusion, ...), kind=kOutput, calls=%fused_computation.17 | convolution fusion | flops 24116696 | bytes 791704 | tf_op jit(solution)/shard_map/lsw,lwe->lse/dot_general | solution.py:43
  150.0 1.6 copy.45
  151.5 1.7 reshape.208
  153.2 1.6 pad_maximum_fusion.3
  154.8 1.6 copy.47
  158.0 2.4 collective-permute-start
  160.4 4.0 %collective-permute-done = bf16[32,8,96]{2,1,0:T(8,128)(2,1)} collective-permute-done((bf16[32,8,96]{2,1,0:T(8,128)(2,1)}, bf16[32,8,96]{2,1,0:T(8,128)(2,1)}, u32[]{:S(2)}, u32[]{:S(2)}) %collective-permute-start) | collective-permute-done | bytes 49184 | tf_op jit(solution)/shard_map/ppermute | solution.py:172
  166.0 2.4 collective-permute-start.1
  168.5 2.5 copy.48
  171.9 22.4 %collective-permute-done.1 = bf16[6144,96]{0,1:T(8,128)(2,1)} collective-permute-done((bf16[6144,96]{0,1:T(8,128)(2,1)}, bf16[6144,96]{0,1:T(8,128)(2,1)}, u32[]{:S(2)}, u32[]{:S(2)}) %collective-permute-start.1) | collective-permute-done | bytes 1179680 | tf_op jit(solution)/shard_map/ppermute | solution.py:168
  194.3 2.5 copy.49
  196.8 53.9 %all-gather.6.cloned.1.call-done = bf16[1024,2,8,96]{3,2,1,0:T(8,128)(2,1)} async-done(((bf16[32,2,8,96]{3,2,1,0:T(8,128)(2,1)}), bf16[1024,2,8,96]{3,2,1,0:T(8,128)(2,1)}) %all-gather.6.cloned.1.call-update) | async-done | bytes 3145744 | tf_op jit(solution)/shard_map/all_gather | solution.py:175
  250.7 4.9 %fusion.14 = bf16[32,8,2,96]{3,0,2,1:T(8,128)(2,1)S(1)} fusion(bf16[1,32,2,96,96]{4,3,2,1,0:T(8,128)(2,1)} %bitcast.54, bf16[1,32,2,96,96]{4,3,2,1,0:T(8,128)(2,1)} %bitcast.53, bf16[32,32,2,8,96,1]{4,3,2,1,0,5:T(8,128)(2,1)} %bitcast.59, f32[2,96]{1,0:T(2,128)S(1)} %maximum_convert_fusion.1), kind=kOutput, calls=%fused_computation.16 | convolution fusion | flops 608796672 | bytes 5604096 | tf_op jit(solution)/shard_map/dot_general | solution.py:178
  255.7 15.4 %all_to_all.5 = bf16[32,8,2,96]{3,2,1,0:T(2,128)(2,1)} all-to-all(bf16[32,8,2,96]{3,2,1,0:T(2,128)(2,1)S(1)} %copy.51), channel_id=1, replica_groups=mesh['rep'=8,'x'=4,'z'=8,'yl'=2] {'x','z'}, dimensions={0} | all-to-all | bytes 196608 | tf_op jit(solution)/shard_map/all_to_all | solution.py:188
  271.1 1.7 reshape.212
  272.8 1.7 copy.52
  274.6 1.7 reshape.211
  276.3 1.6 fusion.29
  (61 shorter events, 35.4 us)
Async XLA Ops:
  6.5 109.2 %copy-start = (bf16[6144,288]{0,1:T(8,128)(2,1)S(1)}, bf16[6144,288]{0,1:T(8,128)(2,1)}, u32[]{:S(2)}) copy-start(bf16[6144,288]{0,1:T(8,128)(2,1)} %param.18) | copy-start | bytes 10616836
  6.5 109.2 %all-gather.4.cloned.1.call-start = ((), (), s32[]{:S(2)}) async-start(), calls=%async_computation.1 | async-start | bytes 6488064 | tf_op jit(solution)/shard_map/all_gather | solution.py:110
  20.5 230.2 %all-gather.6.cloned.1.call-start = ((), (), s32[]{:S(2)}) async-start(), calls=%async_computation.2 | async-start | bytes 4325376 | tf_op jit(solution)/shard_map/all_gather | solution.py:175
  24.4 0.6 copy-start.2
  39.3 82.6 %copy-start.3 = (f32[12]{0:T(128)S(1)}, f32[12]{0:T(128)}, u32[]{:S(2)}) copy-start(f32[12]{0:T(128)} %multiply_exponential_fusion) | copy-start | bytes 148
  145.2 0.8 copy-start.1
  158.0 6.5 %collective-permute-start = (bf16[32,8,96]{2,1,0:T(8,128)(2,1)}, bf16[32,8,96]{2,1,0:T(8,128)(2,1)}, u32[]{:S(2)}, u32[]{:S(2)}) collective-permute-start(bf16[32,8,96]{2,1,0:T(8,128)(2,1)} %get-tuple-element.19), channel_id=1, source_target_pairs={{0,1},{1,0},{2,3},{3,2},{4,5},{5,4},{6,7},{7,6},{8,9},{9,8},{10,11... | collective-permute-start | bytes 147464 | tf_op jit(solution)/shard_map/ppermute | solution.py:172
  166.0 28.2 %collective-permute-start.1 = (bf16[6144,96]{0,1:T(8,128)(2,1)}, bf16[6144,96]{0,1:T(8,128)(2,1)}, u32[]{:S(2)}, u32[]{:S(2)}) collective-permute-start(bf16[6144,96]{0,1:T(8,128)(2,1)} %param.20), channel_id=1, source_target_pairs={{0,1},{1,0},{2,3},{3,2},{4,5},{5,4},{6,7},{7,6},{8,9},{9,8},{10,11... | collective-permute-start | bytes 3538952 | tf_op jit(solution)/shard_map/ppermute | solution.py:168
Sparse Core Ops, SparseCore 0:
  20.6 95.0 all-gather.3
  166.2 84.4 all-gather.5

commit v3 on v2

--- a/solution.py
+++ b/solution.py
@@ -110,13 +110,22 @@
     return lax.all_gather(pair, ("x", "z"), axis=0, tiled=True)
 
 
-def gather_heads(block):
-    pair = lax.all_gather(block, "yl", axis=0, tiled=False)
-    every = lax.all_gather(pair, ("x", "z"), axis=0, tiled=False)
-    return every.reshape((-1,) + block.shape)
-
-
-def on_device(
+def ring_stack(block, axis):
+    n = lax.axis_size(axis)
+    here = lax.axis_index(axis)
+    stack = jnp.zeros((n,) + block.shape, block.dtype)
+    stack = lax.dynamic_update_index_in_dim(stack, block, here, 0)
+    ahead = behind = block
+    for step in range(1, n // 2 + 1):
+        ahead = lax.ppermute(ahead, axis, [(i, (i + 1) % n) for i in range(n)])
+        stack = lax.dynamic_update_index_in_dim(stack, ahead, (here - step) % n, 0)
+        if step < n - step:
+            behind = lax.ppermute(behind, axis, [(i, (i - 1) % n) for i in range(n)])
+            stack = lax.dynamic_update_index_in_dim(stack, behind, (here + step) % n, 0)
+    return stack
+
+
+def layer(
     tokens,
     ln_gain,
     ln_bias,
@@ -131,6 +140,7 @@
     decode_lens,
     slot_valid,
 ):
+    other_w = lax.ppermute(w_dense, "yl", [(0, 1), (1, 0)])
     normed = layer_norm(tokens, ln_gain, ln_bias)
     joined = jnp.dot(gather_rows(normed), w_qkv, preferred_element_type=jnp.float32)
     joined = joined + b_qkv.astype(jnp.float32)
@@ -154,25 +164,25 @@
         query, keys, value_matrix, decode_kv[0], decode_kv[1], decode_lens, slot_valid, score_scale
     )
     heads_out = jnp.concatenate([early, late], axis=0)
-    attn = dense_in_pairs(heads_out, w_dense, b_dense)
+    attn = dense_in_pairs(heads_out, w_dense, other_w, b_dense)
     return (attn.astype(jnp.float32) + tokens.astype(jnp.float32)).astype(jnp.bfloat16)
 
 
-def dense_in_pairs(heads_out, w_dense, b_dense):
+def dense_in_pairs(heads_out, w_dense, other_w, b_dense):
     partner = [(0, 1), (1, 0)]
     side = lax.axis_index("yl")
     rows, head = heads_out.shape
     width = w_dense.shape[1]
     groups = lax.axis_index(("x", "z"))
     per_device = rows // (2 * lax.axis_size(("x", "z")))
-    other_w = lax.ppermute(w_dense, "yl", partner)
     by_owner = heads_out.reshape(-1, 2, per_device, head)
     mine = lax.dynamic_index_in_dim(by_owner, side, axis=1, keepdims=False)
     theirs = lax.dynamic_index_in_dim(by_owner, 1 - side, axis=1, keepdims=False)
     got = lax.ppermute(theirs, "yl", partner)
     pair_heads = jnp.stack([mine, got], axis=1)
     pair_heads = jnp.where(side == 0, pair_heads, pair_heads[:, ::-1])
-    every = lax.all_gather(pair_heads, ("x", "z"), axis=0, tiled=False)
+    every = ring_stack(ring_stack(pair_heads, "z"), "x")
+    every = every.reshape((-1,) + pair_heads.shape)
     pairs = every.shape[0]
     w_pair = jnp.stack([w_dense, other_w]).reshape(2, pairs, 2, head, width)
     mixed = lax.dot_general(
@@ -212,5 +222,5 @@
         P("rep", None),
     )
     return jax.shard_map(
-        on_device, mesh=mesh, in_specs=placed, out_specs=P(("rep",) + TP, None), check_vma=False
-    )
+        layer, mesh=mesh, in_specs=placed, out_specs=P(("rep",) + TP, None), check_vma=False
+    )

time: 286 us -> 285 us (level)
  the two profiles are of different devices: /device:TPU:8 before, /device:TPU:16 now
where the time goes in v3:
time: 285 us; the launch traced here: 283 us
  waiting for transfers between devices  113 us (40%)
  local copies, waits for them, and re-layouts  56.6 us (20%)
  starting transfers between devices  38.8 us (14%)
  other arithmetic  29.1 us (10%)
  blocking collectives  20.5 us (7%)
  between operations  13.9 us (5%)
  matrix products  10.5 us (4%)
    all_gather x1, waiting for transfers between devices, gather_rows(): return lax.all_gather(pair, ('x', 'z'), axis=0, tiled=True)  80.3 us
    ppermute x6, waiting for transfers between devices, ring_stack(): ahead = lax.ppermute(ahead, axis, [(i, (i + 1) % n) for i in range(n)])  29.9 us
    ppermute x4, starting transfers between devices, ring_stack(): behind = lax.ppermute(behind, axis, [(i, (i - 1) % n) for i in range(n)])  18.9 us
    all_to_all x1, blocking collectives, dense_in_pairs(): lax.all_to_all(ordered, ('x', 'z'), split_axis=0, concat_axis=0, tiled=True)  15.1 us
    ppermute x6, starting transfers between devices, ring_stack(): ahead = lax.ppermute(ahead, axis, [(i, (i + 1) % n) for i in range(n)])  13.1 us
    unnamed x15, local copies, waits for them, and re-layouts  6.11 us
  transfers between devices with their start and end apart: 13, of which 5 were waited for; matrix products, arithmetic and copies ran while one was open for 13% of the time, Pallas kernels for 0%

profile of v3, /device:TPU:16, one launch (start us, length us, event | category | flops | bytes accessed | tf_op | source)
XLA Modules:
  0.0 282.6 jit_solution(4212898804040878757)
XLA Ops:
  11.3 5.4 %all_gather.6 = bf16[16,6144]{1,0:T(8,128)(2,1)} all-gather(bf16[8,6144]{1,0:T(8,128)(2,1)S(1)} %fusion.21), channel_id=1, replica_groups=mesh['rep'=8,'x'=4,'z'=8,'yl'=2] {'yl'}, dimensions={0}, use_global_device_ids=true | all-gather | bytes 294912 | tf_op jit(solution)/shard_map/all_gather | solution.py:109
  22.9 2.1 gather_fusion.1
  25.0 2.1 gather_fusion.2
  33.6 1.7 broadcast_select_fusion
  35.3 80.3 %all-gather.2.cloned.1.call-done = bf16[512,6144]{1,0:T(8,128)(2,1)} async-done(((bf16[16,6144]{1,0:T(8,128)(2,1)}), bf16[512,6144]{1,0:T(8,128)(2,1)}) %all-gather.2.cloned.1.call-update) | async-done | bytes 6291472 | tf_op jit(solution)/shard_map/all_gather | solution.py:110
  115.6 4.8 %fusion.62 = (bf16[512,288]{0,1:T(8,128)(2,1)S(1)}, f32[512,288]{0,1:T(8,128)S(1)}) fusion(f32[288]{0:T(512)} %convert_element_type.75, bf16[512,6144]{1,0:T(8,128)(2,1)} %all-gather.2.cloned.1.call-done, bf16[6144,288]{0,1:T(8,128)(2,1)S(1)} %copy-done), kind=kOutput, calls=%fused_computation.124 | convolution fusion | flops 1812234240 | bytes 10716288 | tf_op jit(solution)/shard_map/dot_general | solution.py:145
  133.4 1.7 multiply_reduce_fusion
  147.6 2.9 %convolution_convert_fusion = bf16[4,120,96]{1,2,0:T(8,128)(2,1)} fusion(f32[4,120]{1,0:T(4,128)S(1)} %fusion.63, bf16[4,120,96]{1,2,0:T(8,128)(2,1)} %copy.55, bf16[4,128,96]{1,2,0:T(8,128)(2,1)} %get-tuple-element.24, f32[4,120,248]{2,1,0:T(8,128)} %copy-done.3, pred[120,248]{1,0:T(8,128)(4,1)} %iota_compare_fusion, ...), kind=kOutput, calls=%fused_computation.16 | convolution fusion | flops 24116696 | bytes 791704 | tf_op jit(solution)/shard_map/lsw,lwe->lse/dot_general | solution.py:43
  152.1 1.7 reshape.211
  158.6 3.4 %collective-permute-start = (bf16[32,8,96]{2,1,0:T(8,128)(2,1)}, bf16[32,8,96]{2,1,0:T(8,128)(2,1)}, u32[]{:S(2)}, u32[]{:S(2)}) collective-permute-start(bf16[32,8,96]{2,1,0:T(8,128)(2,1)} %get-tuple-element.21), channel_id=1, source_target_pairs={{0,1},{1,0},{2,3},{3,2},{4,5},{5,4},{6,7},{7,6},{8,9},{9,8},{10,11... | collective-permute-start | bytes 147464 | tf_op jit(solution)/shard_map/ppermute | solution.py:181
  162.0 3.1 %collective-permute-done = bf16[32,8,96]{2,1,0:T(8,128)(2,1)} collective-permute-done((bf16[32,8,96]{2,1,0:T(8,128)(2,1)}, bf16[32,8,96]{2,1,0:T(8,128)(2,1)}, u32[]{:S(2)}, u32[]{:S(2)}) %collective-permute-start) | collective-permute-done | bytes 49184 | tf_op jit(solution)/shard_map/ppermute | solution.py:181
  167.8 3.2 %collective-permute-start.1 = (bf16[32,2,8,96]{3,2,1,0:T(8,128)(2,1)}, bf16[32,2,8,96]{3,2,1,0:T(8,128)(2,1)}, u32[]{:S(2)}, u32[]{:S(2)}) collective-permute-start(bf16[32,2,8,96]{3,2,1,0:T(8,128)(2,1)} %get-tuple-element.7), channel_id=1, source_target_pairs={{0,2},{2,4},{4,6},{6,8},{8,10},{10,12},{12,14},{14,0},{1,3},{3,5},... | collective-permute-start | bytes 294920 | tf_op jit(solution)/shard_map/ppermute | solution.py:120
  171.1 3.8 %collective-permute-start.2 = (bf16[32,2,8,96]{3,2,1,0:T(8,128)(2,1)}, bf16[32,2,8,96]{3,2,1,0:T(8,128)(2,1)}, u32[]{:S(2)}, u32[]{:S(2)}) collective-permute-start(bf16[32,2,8,96]{3,2,1,0:T(8,128)(2,1)} %get-tuple-element.7), channel_id=1, source_target_pairs={{0,14},{2,0},{4,2},{6,4},{8,6},{10,8},{12,10},{14,12},{1,15},{3,1}... | collective-permute-start | bytes 294920 | tf_op jit(solution)/shard_map/ppermute | solution.py:123
  174.9 3.4 %collective-permute-start.11 = (bf16[6144,96]{0,1:T(8,128)(2,1)}, bf16[6144,96]{0,1:T(8,128)(2,1)}, u32[]{:S(2)}, u32[]{:S(2)}) collective-permute-start(bf16[6144,96]{0,1:T(8,128)(2,1)} %param.20), channel_id=1, source_target_pairs={{0,1},{1,0},{2,3},{3,2},{4,5},{5,4},{6,7},{7,6},{8,9},{9,8},{10,11... | collective-permute-start | bytes 3538952 | tf_op jit(solution)/shard_map/ppermute | solution.py:143
  178.4 2.0 collective-permute-start.3
  180.5 5.0 %collective-permute-start.4 = (bf16[32,2,8,96]{3,2,1,0:T(8,128)(2,1)}, bf16[32,2,8,96]{3,2,1,0:T(8,128)(2,1)S(1)}, u32[]{:S(2)}, u32[]{:S(2)}) collective-permute-start(bf16[32,2,8,96]{3,2,1,0:T(8,128)(2,1)} %collective-permute-done.2), channel_id=1, source_target_pairs={{0,14},{2,0},{4,2},{6,4},{8,6},{10,8},{12,10},{14,12},{1,15},{3,1}... | collective-permute-start | bytes 294920 | tf_op jit(solution)/shard_map/ppermute | solution.py:123
  188.7 1.9 collective-permute-start.5
  190.6 5.1 %collective-permute-start.6 = (bf16[32,2,8,96]{3,2,1,0:T(8,128)(2,1)S(1)}, bf16[32,2,8,96]{3,2,1,0:T(8,128)(2,1)S(1)}, u32[]{:S(2)}, u32[]{:S(2)}) collective-permute-start(bf16[32,2,8,96]{3,2,1,0:T(8,128)(2,1)S(1)} %collective-permute-done.4), channel_id=1, source_target_pairs={{0,14},{2,0},{4,2},{6,4},{8,6},{10,8},{12,10},{14,12},{1,15},{3,1}... | collective-permute-start | bytes 294920 | tf_op jit(solution)/shard_map/ppermute | solution.py:123
  197.1 1.9 collective-permute-start.7
  200.3 4.8 %collective-permute-done.7 = bf16[32,2,8,96]{3,2,1,0:T(8,128)(2,1)S(1)} collective-permute-done((bf16[32,2,8,96]{3,2,1,0:T(8,128)(2,1)S(1)}, bf16[32,2,8,96]{3,2,1,0:T(8,128)(2,1)S(1)}, u32[]{:S(2)}, u32[]{:S(2)}) %collective-permute-start.7) | collective-permute-done | bytes 98336 | tf_op jit(solution)/shard_map/ppermute | solution.py:120
  205.8 2.1 collective-permute-start.8
  207.9 4.9 %collective-permute-start.9 = (bf16[8,32,2,8,96]{4,3,2,1,0:T(8,128)(2,1)}, bf16[8,32,2,8,96]{4,3,2,1,0:T(8,128)(2,1)}, u32[]{:S(2)}, u32[]{:S(2)}) collective-permute-start(bf16[8,32,2,8,96]{4,3,2,1,0:T(8,128)(2,1)} %bitcast_dynamic-update-slice_fusion), channel_id=1, source_target_pairs={{0,48},{16,0},{32,16},{48,32},{1,49},{17,1},{33,17},{49,33},{2,50}... | collective-permute-start | bytes 2359304 | tf_op jit(solution)/shard_map/ppermute | solution.py:123
  212.9 2.5 copy.63
  216.3 2.5 copy.64
  218.9 10.4 %collective-permute-done.8 = bf16[8,32,2,8,96]{4,3,2,1,0:T(8,128)(2,1)} collective-permute-done((bf16[8,32,2,8,96]{4,3,2,1,0:T(8,128)(2,1)}, bf16[8,32,2,8,96]{4,3,2,1,0:T(8,128)(2,1)}, u32[]{:S(2)}, u32[]{:S(2)}) %collective-permute-start.8) | collective-permute-done | bytes 786464 | tf_op jit(solution)/shard_map/ppermute | solution.py:120
  229.3 1.9 collective-permute-start.10
  232.3 1.7 copy_dynamic-update-slice_fusion.3
  237.2 14.7 %collective-permute-done.10 = bf16[8,32,2,8,96]{4,3,2,1,0:T(8,128)(2,1)S(1)} collective-permute-done((bf16[8,32,2,8,96]{4,3,2,1,0:T(8,128)(2,1)}, bf16[8,32,2,8,96]{4,3,2,1,0:T(8,128)(2,1)S(1)}, u32[]{:S(2)}, u32[]{:S(2)}) %collective-permute-start.10) | collective-permute-done | bytes 786464 | tf_op jit(solution)/shard_map/ppermute | solution.py:120
  253.9 15.1 %all_to_all.5 = bf16[32,8,2,96]{3,2,1,0:T(2,128)(2,1)} all-to-all(bf16[32,8,2,96]{3,2,1,0:T(2,128)(2,1)S(1)} %copy.65), channel_id=1, replica_groups=mesh['rep'=8,'x'=4,'z'=8,'yl'=2] {'x','z'}, dimensions={0} | all-to-all | bytes 196608 | tf_op jit(solution)/shard_map/all_to_all | solution.py:198
  269.0 1.7 reshape.216
  270.7 1.7 copy.66
  272.4 1.7 reshape.215
  (95 shorter events, 67.2 us)
Async XLA Ops:
  6.5 109.1 %copy-start = (bf16[6144,288]{0,1:T(8,128)(2,1)S(1)}, bf16[6144,288]{0,1:T(8,128)(2,1)}, u32[]{:S(2)}) copy-start(bf16[6144,288]{0,1:T(8,128)(2,1)} %param.18) | copy-start | bytes 10616836
  6.5 109.1 %all-gather.2.cloned.1.call-start = ((), (), s32[]{:S(2)}) async-start(), calls=%async_computation.1 | async-start | bytes 6488064 | tf_op jit(solution)/shard_map/all_gather | solution.py:110
  19.4 0.5 copy-start.4
  35.3 85.8 %copy-start.5 = (f32[12]{0:T(128)S(1)}, f32[12]{0:T(128)}, u32[]{:S(2)}) copy-start(f32[12]{0:T(128)} %multiply_exponential_fusion) | copy-start | bytes 148
  145.7 0.8 copy-start.3
  158.6 6.5 %collective-permute-start = (bf16[32,8,96]{2,1,0:T(8,128)(2,1)}, bf16[32,8,96]{2,1,0:T(8,128)(2,1)}, u32[]{:S(2)}, u32[]{:S(2)}) collective-permute-start(bf16[32,8,96]{2,1,0:T(8,128)(2,1)} %get-tuple-element.21), channel_id=1, source_target_pairs={{0,1},{1,0},{2,3},{3,2},{4,5},{5,4},{6,7},{7,6},{8,9},{9,8},{10,11... | collective-permute-start | bytes 147464 | tf_op jit(solution)/shard_map/ppermute | solution.py:181
  167.8 10.6 %collective-permute-start.1 = (bf16[32,2,8,96]{3,2,1,0:T(8,128)(2,1)}, bf16[32,2,8,96]{3,2,1,0:T(8,128)(2,1)}, u32[]{:S(2)}, u32[]{:S(2)}) collective-permute-start(bf16[32,2,8,96]{3,2,1,0:T(8,128)(2,1)} %get-tuple-element.7), channel_id=1, source_target_pairs={{0,2},{2,4},{4,6},{6,8},{8,10},{10,12},{12,14},{14,0},{1,3},{3,5},... | collective-permute-start | bytes 294920 | tf_op jit(solution)/shard_map/ppermute | solution.py:120
  171.1 9.4 %collective-permute-start.2 = (bf16[32,2,8,96]{3,2,1,0:T(8,128)(2,1)}, bf16[32,2,8,96]{3,2,1,0:T(8,128)(2,1)}, u32[]{:S(2)}, u32[]{:S(2)}) collective-permute-start(bf16[32,2,8,96]{3,2,1,0:T(8,128)(2,1)} %get-tuple-element.7), channel_id=1, source_target_pairs={{0,14},{2,0},{4,2},{6,4},{8,6},{10,8},{12,10},{14,12},{1,15},{3,1}... | collective-permute-start | bytes 294920 | tf_op jit(solution)/shard_map/ppermute | solution.py:123
  174.9 41.4 %collective-permute-start.11 = (bf16[6144,96]{0,1:T(8,128)(2,1)}, bf16[6144,96]{0,1:T(8,128)(2,1)}, u32[]{:S(2)}, u32[]{:S(2)}) collective-permute-start(bf16[6144,96]{0,1:T(8,128)(2,1)} %param.20), channel_id=1, source_target_pairs={{0,1},{1,0},{2,3},{3,2},{4,5},{5,4},{6,7},{7,6},{8,9},{9,8},{10,11... | collective-permute-start | bytes 3538952 | tf_op jit(solution)/shard_map/ppermute | solution.py:143
  178.4 10.2 %collective-permute-start.3 = (bf16[32,2,8,96]{3,2,1,0:T(8,128)(2,1)}, bf16[32,2,8,96]{3,2,1,0:T(8,128)(2,1)S(1)}, u32[]{:S(2)}, u32[]{:S(2)}) collective-permute-start(bf16[32,2,8,96]{3,2,1,0:T(8,128)(2,1)} %collective-permute-done.1), channel_id=1, source_target_pairs={{0,2},{2,4},{4,6},{6,8},{8,10},{10,12},{12,14},{14,0},{1,3},{3,5},... | collective-permute-start | bytes 294920 | tf_op jit(solution)/shard_map/ppermute | solution.py:120
  180.5 10.1 %collective-permute-start.4 = (bf16[32,2,8,96]{3,2,1,0:T(8,128)(2,1)}, bf16[32,2,8,96]{3,2,1,0:T(8,128)(2,1)S(1)}, u32[]{:S(2)}, u32[]{:S(2)}) collective-permute-start(bf16[32,2,8,96]{3,2,1,0:T(8,128)(2,1)} %collective-permute-done.2), channel_id=1, source_target_pairs={{0,14},{2,0},{4,2},{6,4},{8,6},{10,8},{12,10},{14,12},{1,15},{3,1}... | collective-permute-start | bytes 294920 | tf_op jit(solution)/shard_map/ppermute | solution.py:123
  188.7 8.4 %collective-permute-start.5 = (bf16[32,2,8,96]{3,2,1,0:T(8,128)(2,1)S(1)}, bf16[32,2,8,96]{3,2,1,0:T(8,128)(2,1)S(1)}, u32[]{:S(2)}, u32[]{:S(2)}) collective-permute-start(bf16[32,2,8,96]{3,2,1,0:T(8,128)(2,1)S(1)} %collective-permute-done.3), channel_id=1, source_target_pairs={{0,2},{2,4},{4,6},{6,8},{8,10},{10,12},{12,14},{14,0},{1,3},{3,5},... | collective-permute-start | bytes 294920 | tf_op jit(solution)/shard_map/ppermute | solution.py:120
  190.6 9.1 %collective-permute-start.6 = (bf16[32,2,8,96]{3,2,1,0:T(8,128)(2,1)S(1)}, bf16[32,2,8,96]{3,2,1,0:T(8,128)(2,1)S(1)}, u32[]{:S(2)}, u32[]{:S(2)}) collective-permute-start(bf16[32,2,8,96]{3,2,1,0:T(8,128)(2,1)S(1)} %collective-permute-done.4), channel_id=1, source_target_pairs={{0,14},{2,0},{4,2},{6,4},{8,6},{10,8},{12,10},{14,12},{1,15},{3,1}... | collective-permute-start | bytes 294920 | tf_op jit(solution)/shard_map/ppermute | solution.py:123
  197.1 8.1 %collective-permute-start.7 = (bf16[32,2,8,96]{3,2,1,0:T(8,128)(2,1)S(1)}, bf16[32,2,8,96]{3,2,1,0:T(8,128)(2,1)S(1)}, u32[]{:S(2)}, u32[]{:S(2)}) collective-permute-start(bf16[32,2,8,96]{3,2,1,0:T(8,128)(2,1)S(1)} %collective-permute-done.5), channel_id=1, source_target_pairs={{0,2},{2,4},{4,6},{6,8},{8,10},{10,12},{12,14},{14,0},{1,3},{3,5},... | collective-permute-start | bytes 294920 | tf_op jit(solution)/shard_map/ppermute | solution.py:120
  205.8 23.5 %collective-permute-start.8 = (bf16[8,32,2,8,96]{4,3,2,1,0:T(8,128)(2,1)}, bf16[8,32,2,8,96]{4,3,2,1,0:T(8,128)(2,1)}, u32[]{:S(2)}, u32[]{:S(2)}) collective-permute-start(bf16[8,32,2,8,96]{4,3,2,1,0:T(8,128)(2,1)} %bitcast_dynamic-update-slice_fusion), channel_id=1, source_target_pairs={{0,16},{16,32},{32,48},{48,0},{1,17},{17,33},{33,49},{49,1},{2,18}... | collective-permute-start | bytes 2359304 | tf_op jit(solution)/shard_map/ppermute | solution.py:120
  207.9 27.7 %collective-permute-start.9 = (bf16[8,32,2,8,96]{4,3,2,1,0:T(8,128)(2,1)}, bf16[8,32,2,8,96]{4,3,2,1,0:T(8,128)(2,1)}, u32[]{:S(2)}, u32[]{:S(2)}) collective-permute-start(bf16[8,32,2,8,96]{4,3,2,1,0:T(8,128)(2,1)} %bitcast_dynamic-update-slice_fusion), channel_id=1, source_target_pairs={{0,48},{16,0},{32,16},{48,32},{1,49},{17,1},{33,17},{49,33},{2,50}... | collective-permute-start | bytes 2359304 | tf_op jit(solution)/shard_map/ppermute | solution.py:123
  229.3 22.5 %collective-permute-start.10 = (bf16[8,32,2,8,96]{4,3,2,1,0:T(8,128)(2,1)}, bf16[8,32,2,8,96]{4,3,2,1,0:T(8,128)(2,1)S(1)}, u32[]{:S(2)}, u32[]{:S(2)}) collective-permute-start(bf16[8,32,2,8,96]{4,3,2,1,0:T(8,128)(2,1)} %collective-permute-done.8), channel_id=1, source_target_pairs={{0,16},{16,32},{32,48},{48,0},{1,17},{17,33},{33,49},{49,1},{2,18}... | collective-permute-start | bytes 2359304 | tf_op jit(solution)/shard_map/ppermute | solution.py:120
  232.3 19.9 %copy-start.1 = (bf16[6144,96]{1,0:T(8,128)(2,1)S(1)}, bf16[6144,96]{1,0:T(8,128)(2,1)}, u32[]{:S(2)}) copy-start(bf16[6144,96]{1,0:T(8,128)(2,1)} %copy.63) | copy-start | bytes 3538948
  232.3 19.9 %copy-start.2 = (bf16[6144,96]{1,0:T(8,128)(2,1)S(1)}, bf16[6144,96]{1,0:T(8,128)(2,1)}, u32[]{:S(2)}) copy-start(bf16[6144,96]{1,0:T(8,128)(2,1)} %copy.64) | copy-start | bytes 3538948
Sparse Core Ops, SparseCore 0:
  16.8 98.7 all-gather.1

commit v4 on v3

--- a/solution.py
+++ b/solution.py
@@ -108,21 +108,6 @@
 def gather_rows(block):
     pair = lax.all_gather(block, "yl", axis=0, tiled=True)
     return lax.all_gather(pair, ("x", "z"), axis=0, tiled=True)
-
-
-def ring_stack(block, axis):
-    n = lax.axis_size(axis)
-    here = lax.axis_index(axis)
-    stack = jnp.zeros((n,) + block.shape, block.dtype)
-    stack = lax.dynamic_update_index_in_dim(stack, block, here, 0)
-    ahead = behind = block
-    for step in range(1, n // 2 + 1):
-        ahead = lax.ppermute(ahead, axis, [(i, (i + 1) % n) for i in range(n)])
-        stack = lax.dynamic_update_index_in_dim(stack, ahead, (here - step) % n, 0)
-        if step < n - step:
-            behind = lax.ppermute(behind, axis, [(i, (i - 1) % n) for i in range(n)])
-            stack = lax.dynamic_update_index_in_dim(stack, behind, (here + step) % n, 0)
-    return stack
 
 
 def layer(
@@ -181,7 +166,8 @@
     got = lax.ppermute(theirs, "yl", partner)
     pair_heads = jnp.stack([mine, got], axis=1)
     pair_heads = jnp.where(side == 0, pair_heads, pair_heads[:, ::-1])
-    every = ring_stack(ring_stack(pair_heads, "z"), "x")
+    along_z = lax.all_gather(pair_heads, "z", axis=0, tiled=False)
+    every = lax.all_gather(along_z, "x", axis=0, tiled=False)
     every = every.reshape((-1,) + pair_heads.shape)
     pairs = every.shape[0]
     w_pair = jnp.stack([w_dense, other_w]).reshape(2, pairs, 2, head, width)

time: 285 us -> 284 us (level)
  the two profiles are of different devices: /device:TPU:16 before, /device:TPU:8 now
where the time goes in v4:
time: 284 us; the launch traced here: 282 us
  waiting for transfers between devices  123 us (43%)
  blocking collectives  55.4 us (20%)
  local copies, waits for them, and re-layouts  44.1 us (16%)
  other arithmetic  27.8 us (10%)
  matrix products  13.5 us (5%)
  between operations  13.5 us (5%)
  starting transfers between devices  4.93 us (2%)
    all_gather x1, waiting for transfers between devices, gather_rows(): return lax.all_gather(pair, ('x', 'z'), axis=0, tiled=True)  76.4 us
    all_gather x1, blocking collectives, dense_in_pairs(): along_z = lax.all_gather(pair_heads, 'z', axis=0, tiled=False)  26.8 us
    all_gather x1, waiting for transfers between devices, dense_in_pairs(): every = lax.all_gather(along_z, 'x', axis=0, tiled=False)  25.1 us
    all_to_all x1, blocking collectives, dense_in_pairs(): lax.all_to_all(ordered, ('x', 'z'), split_axis=0, concat_axis=0, tiled=True)  19.4 us
    ppermute x1, waiting for transfers between devices, layer(): other_w = lax.ppermute(w_dense, 'yl', [(0, 1), (1, 0)])  17 us
    all_gather x1, blocking collectives, gather_rows(): pair = lax.all_gather(block, 'yl', axis=0, tiled=True)  9.15 us
    unnamed x11, local copies, waits for them, and re-layouts  6.17 us
  transfers between devices with their start and end apart: 4, of which 4 were waited for; matrix products, arithmetic and copies ran while one was open for 9% of the time, Pallas kernels for 0%

profile of v4, /device:TPU:8, one launch (start us, length us, event | category | flops | bytes accessed | tf_op | source)
XLA Modules:
  0.0 281.9 jit_solution(5862714593577762733)
XLA Ops:
  11.3 9.1 %all_gather.18 = bf16[16,6144]{1,0:T(8,128)(2,1)} all-gather(bf16[8,6144]{1,0:T(8,128)(2,1)S(1)} %fusion.28), channel_id=1, replica_groups=mesh['rep'=8,'x'=4,'z'=8,'yl'=2] {'yl'}, dimensions={0}, use_global_device_ids=true | all-gather | bytes 294912 | tf_op jit(solution)/shard_map/all_gather | solution.py:109
  25.2 1.6 slice_bitcast_fusion.1
  26.8 2.1 gather_fusion.2
  28.9 2.1 gather_fusion.1
  36.0 1.6 slice_bitcast_fusion
  37.6 1.7 broadcast_select_fusion
  39.3 76.4 %all-gather.5.cloned.1.call-done = bf16[512,6144]{1,0:T(8,128)(2,1)} async-done(((bf16[16,6144]{1,0:T(8,128)(2,1)}), bf16[512,6144]{1,0:T(8,128)(2,1)}) %all-gather.5.cloned.1.call-update) | async-done | bytes 6291472 | tf_op jit(solution)/shard_map/all_gather | solution.py:110
  115.7 4.8 %fusion.69 = (bf16[512,288]{0,1:T(8,128)(2,1)S(1)}, f32[512,288]{0,1:T(8,128)S(1)}) fusion(f32[288]{0:T(512)} %convert_element_type.75, bf16[512,6144]{1,0:T(8,128)(2,1)} %all-gather.5.cloned.1.call-done, bf16[6144,288]{0,1:T(8,128)(2,1)S(1)} %copy-done), kind=kOutput, calls=%fused_computation.113 | convolution fusion | flops 1812234240 | bytes 10716288 | tf_op jit(solution)/shard_map/dot_general | solution.py:130
  124.9 1.6 reshape.210
  128.1 1.6 reshape.208
  129.7 1.6 reshape.209
  131.4 1.5 copy.42
  140.8 1.7 multiply_reduce_fusion
  147.1 2.9 %convolution_convert_fusion = bf16[4,120,96]{1,2,0:T(8,128)(2,1)} fusion(f32[4,120]{1,0:T(4,128)S(1)} %fusion.70, bf16[4,120,96]{1,2,0:T(8,128)(2,1)} %copy.44, bf16[4,128,96]{1,2,0:T(8,128)(2,1)} %get-tuple-element.22, f32[4,120,248]{2,1,0:T(8,128)} %copy-done.1, pred[120,248]{1,0:T(8,128)(4,1)} %iota_compare_fusion, ...), kind=kOutput, calls=%fused_computation.17 | convolution fusion | flops 24116696 | bytes 791704 | tf_op jit(solution)/shard_map/lsw,lwe->lse/dot_general | solution.py:43
  150.0 1.6 copy.45
  151.5 1.7 reshape.211
  153.2 1.6 pad_maximum_fusion.3
  154.8 1.6 copy.47
  158.0 2.4 collective-permute-start
  160.4 4.0 %collective-permute-done = bf16[32,8,96]{2,1,0:T(8,128)(2,1)} collective-permute-done((bf16[32,8,96]{2,1,0:T(8,128)(2,1)}, bf16[32,8,96]{2,1,0:T(8,128)(2,1)}, u32[]{:S(2)}, u32[]{:S(2)}) %collective-permute-start) | collective-permute-done | bytes 49184 | tf_op jit(solution)/shard_map/ppermute | solution.py:166
  165.4 26.8 %all-gather = bf16[256,2,8,96]{3,2,1,0:T(8,128)(2,1)S(1)} all-gather(bf16[32,2,8,96]{3,2,1,0:T(8,128)(2,1)S(1)} %reverse_select_fusion.1), channel_id=2, replica_groups=mesh['rep'=8,'x'=4,'z'=8,'yl'=2] {'z'}, dimensions={0}, use_global_device_ids=true | all-gather | bytes 884736 | tf_op jit(solution)/shard_map/all_gather | solution.py:169
  193.5 2.4 collective-permute-start.1
  196.0 2.5 copy.49
  199.4 17.0 %collective-permute-done.1 = bf16[6144,96]{0,1:T(8,128)(2,1)} collective-permute-done((bf16[6144,96]{0,1:T(8,128)(2,1)}, bf16[6144,96]{0,1:T(8,128)(2,1)}, u32[]{:S(2)}, u32[]{:S(2)}) %collective-permute-start.1) | collective-permute-done | bytes 1179680 | tf_op jit(solution)/shard_map/ppermute | solution.py:128
  216.4 2.6 copy.50
  218.9 25.1 %all-gather.7.cloned.1.call-done = bf16[32,32,2,8,96]{4,1,2,0,3:T(8,128)(2,1)} async-done(((bf16[8,32,2,8,96]{4,1,2,0,3:T(8,128)(2,1)}), bf16[32,32,2,8,96]{4,1,2,0,3:T(8,128)(2,1)}) %all-gather.7.cloned.1.call-update) | async-done | bytes 3145744 | tf_op jit(solution)/shard_map/all_gather | solution.py:170
  244.0 4.6 %fusion.14 = bf16[32,8,2,96]{3,0,2,1:T(8,128)(2,1)S(1)} fusion(bf16[1,32,2,96,96]{4,3,2,1,0:T(8,128)(2,1)} %bitcast.64, bf16[1,32,2,96,96]{4,3,2,1,0:T(8,128)(2,1)} %bitcast.63, bf16[32,32,2,8,96]{4,1,2,0,3:T(8,128)(2,1)} %all-gather.7.cloned.1.call-done, f32[2,96]{1,0:T(2,128)S(1)} %maximum_convert_fusion.1), kind=kOutput, calls=%fused_computation.16 | convolution fusion | flops 608796672 | bytes 5604096 | tf_op jit(solution)/shard_map/dot_general | solution.py:174
  248.8 19.4 %all_to_all.5 = bf16[32,8,2,96]{3,2,1,0:T(2,128)(2,1)} all-to-all(bf16[32,8,2,96]{3,2,1,0:T(2,128)(2,1)S(1)} %copy.51), channel_id=1, replica_groups=mesh['rep'=8,'x'=4,'z'=8,'yl'=2] {'x','z'}, dimensions={0} | all-to-all | bytes 196608 | tf_op jit(solution)/shard_map/all_to_all | solution.py:184
  268.2 1.7 reshape.216
  269.9 1.7 copy.52
  271.7 1.7 reshape.215
  273.4 1.6 fusion.29
  (63 shorter events, 37.6 us)
Async XLA Ops:
  6.5 109.2 %copy-start = (bf16[6144,288]{0,1:T(8,128)(2,1)S(1)}, bf16[6144,288]{0,1:T(8,128)(2,1)}, u32[]{:S(2)}) copy-start(bf16[6144,288]{0,1:T(8,128)(2,1)} %param.18) | copy-start | bytes 10616836
  6.5 109.2 %all-gather.5.cloned.1.call-start = ((), (), s32[]{:S(2)}) async-start(), calls=%async_computation.1 | async-start | bytes 6488064 | tf_op jit(solution)/shard_map/all_gather | solution.py:110
  20.5 223.6 %all-gather.7.cloned.1.call-start = ((), (), s32[]{:S(2)}) async-start(), calls=%async_computation.2 | async-start | bytes 5242880 | tf_op jit(solution)/shard_map/all_gather | solution.py:170
  24.4 0.6 copy-start.2
  39.3 82.6 %copy-start.3 = (f32[12]{0:T(128)S(1)}, f32[12]{0:T(128)}, u32[]{:S(2)}) copy-start(f32[12]{0:T(128)} %multiply_exponential_fusion) | copy-start | bytes 148
  145.2 0.8 copy-start.1
  158.0 6.5 %collective-permute-start = (bf16[32,8,96]{2,1,0:T(8,128)(2,1)}, bf16[32,8,96]{2,1,0:T(8,128)(2,1)}, u32[]{:S(2)}, u32[]{:S(2)}) collective-permute-start(bf16[32,8,96]{2,1,0:T(8,128)(2,1)} %get-tuple-element.19), channel_id=1, source_target_pairs={{0,1},{1,0},{2,3},{3,2},{4,5},{5,4},{6,7},{7,6},{8,9},{9,8},{10,11... | collective-permute-start | bytes 147464 | tf_op jit(solution)/shard_map/ppermute | solution.py:166
  193.5 22.9 %collective-permute-start.1 = (bf16[6144,96]{0,1:T(8,128)(2,1)}, bf16[6144,96]{0,1:T(8,128)(2,1)}, u32[]{:S(2)}, u32[]{:S(2)}) collective-permute-start(bf16[6144,96]{0,1:T(8,128)(2,1)} %param.20), channel_id=1, source_target_pairs={{0,1},{1,0},{2,3},{3,2},{4,5},{5,4},{6,7},{7,6},{8,9},{9,8},{10,11... | collective-permute-start | bytes 3538952 | tf_op jit(solution)/shard_map/ppermute | solution.py:128
Sparse Core Ops, SparseCore 0:
  20.6 95.0 all-gather.4
  193.6 50.3 all-gather.6

commit v5 on v2

--- a/solution.py
+++ b/solution.py
@@ -185,8 +185,9 @@
     own_first = jnp.stack([bias[side], bias[1 - side]]).astype(jnp.float32)
     attn = (mixed + own_first).astype(jnp.bfloat16)
     ordered = jnp.where(side == 0, attn, attn[:, :, ::-1])
-    own_rows = lax.all_to_all(ordered, ("x", "z"), split_axis=0, concat_axis=0, tiled=True)
-    return jnp.transpose(own_rows.reshape(pairs, per_device, 2 * width), (1, 0, 2)).reshape(per_device, -1)
+    ordered = ordered.reshape(pairs, per_device, 1, 2 * width)
+    own_rows = lax.all_to_all(ordered, ("x", "z"), split_axis=0, concat_axis=2, tiled=True)
+    return own_rows.reshape(per_device, -1)
 
 
 def solution(mesh):

time: 286 us -> 286 us (level)
  no operation moved by 1% of the time
where the time goes in v5:
time: 286 us; the launch traced here: 285 us
  waiting for transfers between devices  157 us (55%)
  local copies, waits for them, and re-layouts  42.4 us (15%)
  other arithmetic  28.5 us (10%)
  blocking collectives  24.7 us (9%)
  matrix products  13.8 us (5%)
  between operations  13.5 us (5%)
  starting transfers between devices  4.92 us (2%)
    all_gather x1, waiting for transfers between devices, gather_rows(): return lax.all_gather(pair, ('x', 'z'), axis=0, tiled=True)  76.4 us
    all_gather x1, waiting for transfers between devices, dense_in_pairs(): every = lax.all_gather(pair_heads, ('x', 'z'), axis=0, tiled=False)  53.9 us
    ppermute x1, waiting for transfers between devices, dense_in_pairs(): other_w = lax.ppermute(w_dense, 'yl', partner)  22.4 us
    all_to_all x1, blocking collectives, dense_in_pairs(): lax.all_to_all(ordered, ('x', 'z'), split_axis=0, concat_axis=2, tiled=True)  15.5 us
    all_gather x1, blocking collectives, gather_rows(): pair = lax.all_gather(block, 'yl', axis=0, tiled=True)  9.15 us
    unnamed x11, local copies, waits for them, and re-layouts  6.17 us
  transfers between devices with their start and end apart: 4, of which 4 were waited for; matrix products, arithmetic and copies ran while one was open for 8% of the time, Pallas kernels for 0%

profile of v5, /device:TPU:8, one launch (start us, length us, event | category | flops | bytes accessed | tf_op | source)
XLA Modules:
  0.0 284.6 jit_solution(17618555543978148283)
XLA Ops:
  11.3 9.1 %all_gather.12 = bf16[16,6144]{1,0:T(8,128)(2,1)} all-gather(bf16[8,6144]{1,0:T(8,128)(2,1)S(1)} %fusion.28), channel_id=1, replica_groups=mesh['rep'=8,'x'=4,'z'=8,'yl'=2] {'yl'}, dimensions={0}, use_global_device_ids=true | all-gather | bytes 294912 | tf_op jit(solution)/shard_map/all_gather | solution.py:109
  25.2 1.6 slice_bitcast_fusion.1
  26.8 2.1 gather_fusion.2
  28.9 2.1 gather_fusion.1
  36.0 1.6 slice_bitcast_fusion
  37.6 1.7 broadcast_select_fusion
  39.3 76.4 %all-gather.4.cloned.1.call-done = bf16[512,6144]{1,0:T(8,128)(2,1)} async-done(((bf16[16,6144]{1,0:T(8,128)(2,1)}), bf16[512,6144]{1,0:T(8,128)(2,1)}) %all-gather.4.cloned.1.call-update) | async-done | bytes 6291472 | tf_op jit(solution)/shard_map/all_gather | solution.py:110
  115.7 4.8 %fusion.69 = (bf16[512,288]{0,1:T(8,128)(2,1)S(1)}, f32[512,288]{0,1:T(8,128)S(1)}) fusion(f32[288]{0:T(512)} %convert_element_type.75, bf16[512,6144]{1,0:T(8,128)(2,1)} %all-gather.4.cloned.1.call-done, bf16[6144,288]{0,1:T(8,128)(2,1)S(1)} %copy-done), kind=kOutput, calls=%fused_computation.114 | convolution fusion | flops 1812234240 | bytes 10716288 | tf_op jit(solution)/shard_map/dot_general | solution.py:135
  124.9 1.6 reshape.210
  126.6 1.5 copy.44
  128.1 1.6 reshape.208
  129.7 1.6 reshape.209
  131.4 1.5 copy.42
  140.8 1.7 multiply_reduce_fusion
  147.1 2.9 %convolution_convert_fusion = bf16[4,120,96]{1,2,0:T(8,128)(2,1)} fusion(f32[4,120]{1,0:T(4,128)S(1)} %fusion.70, bf16[4,120,96]{1,2,0:T(8,128)(2,1)} %copy.44, bf16[4,128,96]{1,2,0:T(8,128)(2,1)} %get-tuple-element.22, f32[4,120,248]{2,1,0:T(8,128)} %copy-done.1, pred[120,248]{1,0:T(8,128)(4,1)} %iota_compare_fusion, ...), kind=kOutput, calls=%fused_computation.17 | convolution fusion | flops 24116696 | bytes 791704 | tf_op jit(solution)/shard_map/lsw,lwe->lse/dot_general | solution.py:43
  150.0 1.6 copy.45
  151.5 1.7 reshape.211
  153.2 1.6 pad_maximum_fusion.3
  154.8 1.6 copy.47
  156.5 1.5 constant_dynamic-slice_fusion.2
  158.0 2.4 collective-permute-start
  160.4 4.0 %collective-permute-done = bf16[32,8,96]{2,1,0:T(8,128)(2,1)} collective-permute-done((bf16[32,8,96]{2,1,0:T(8,128)(2,1)}, bf16[32,8,96]{2,1,0:T(8,128)(2,1)}, u32[]{:S(2)}, u32[]{:S(2)}) %collective-permute-start) | collective-permute-done | bytes 49184 | tf_op jit(solution)/shard_map/ppermute | solution.py:172
  166.0 2.4 collective-permute-start.1
  168.5 2.5 copy.48
  171.9 22.4 %collective-permute-done.1 = bf16[6144,96]{0,1:T(8,128)(2,1)} collective-permute-done((bf16[6144,96]{0,1:T(8,128)(2,1)}, bf16[6144,96]{0,1:T(8,128)(2,1)}, u32[]{:S(2)}, u32[]{:S(2)}) %collective-permute-start.1) | collective-permute-done | bytes 1179680 | tf_op jit(solution)/shard_map/ppermute | solution.py:168
  194.3 2.5 copy.49
  196.8 53.9 %all-gather.6.cloned.1.call-done = bf16[1024,2,8,96]{3,2,1,0:T(8,128)(2,1)} async-done(((bf16[32,2,8,96]{3,2,1,0:T(8,128)(2,1)}), bf16[1024,2,8,96]{3,2,1,0:T(8,128)(2,1)}) %all-gather.6.cloned.1.call-update) | async-done | bytes 3145744 | tf_op jit(solution)/shard_map/all_gather | solution.py:175
  250.7 4.9 %fusion.14 = bf16[32,8,2,96]{3,0,2,1:T(8,128)(2,1)S(1)} fusion(bf16[1,32,2,96,96]{4,3,2,1,0:T(8,128)(2,1)} %bitcast.63, bf16[1,32,2,96,96]{4,3,2,1,0:T(8,128)(2,1)} %bitcast.62, bf16[32,32,2,8,96,1]{4,3,2,1,0,5:T(8,128)(2,1)} %bitcast.68, f32[2,96]{1,0:T(2,128)S(1)} %maximum_convert_fusion.1), kind=kOutput, calls=%fused_computation.16 | convolution fusion | flops 608796672 | bytes 5604096 | tf_op jit(solution)/shard_map/dot_general | solution.py:178
  256.3 1.7 reshape.214
  258.0 15.5 %all_to_all.4 = bf16[32,8,1,192]{3,1,2,0:T(8,128)(2,1)S(1)} all-to-all(bf16[32,8,1,192]{3,1,2,0:T(8,128)(2,1)} %bitcast.65), channel_id=1, replica_groups=mesh['rep'=8,'x'=4,'z'=8,'yl'=2] {'x','z'}, dimensions={0} | all-to-all | bytes 196608 | tf_op jit(solution)/shard_map/all_to_all | solution.py:189
  274.3 1.8 reshape.215
  276.1 1.6 fusion.29
  (62 shorter events, 35.3 us)
Async XLA Ops:
  6.5 109.2 %copy-start = (bf16[6144,288]{0,1:T(8,128)(2,1)S(1)}, bf16[6144,288]{0,1:T(8,128)(2,1)}, u32[]{:S(2)}) copy-start(bf16[6144,288]{0,1:T(8,128)(2,1)} %param.18) | copy-start | bytes 10616836
  6.5 109.2 %all-gather.4.cloned.1.call-start = ((), (), s32[]{:S(2)}) async-start(), calls=%async_computation.1 | async-start | bytes 6488064 | tf_op jit(solution)/shard_map/all_gather | solution.py:110
  20.5 230.2 %all-gather.6.cloned.1.call-start = ((), (), s32[]{:S(2)}) async-start(), calls=%async_computation.2 | async-start | bytes 4325376 | tf_op jit(solution)/shard_map/all_gather | solution.py:175
  24.4 0.6 copy-start.2
  39.3 82.6 %copy-start.3 = (f32[12]{0:T(128)S(1)}, f32[12]{0:T(128)}, u32[]{:S(2)}) copy-start(f32[12]{0:T(128)} %multiply_exponential_fusion) | copy-start | bytes 148
  145.2 0.8 copy-start.1
  158.0 6.5 %collective-permute-start = (bf16[32,8,96]{2,1,0:T(8,128)(2,1)}, bf16[32,8,96]{2,1,0:T(8,128)(2,1)}, u32[]{:S(2)}, u32[]{:S(2)}) collective-permute-start(bf16[32,8,96]{2,1,0:T(8,128)(2,1)} %get-tuple-element.19), channel_id=1, source_target_pairs={{0,1},{1,0},{2,3},{3,2},{4,5},{5,4},{6,7},{7,6},{8,9},{9,8},{10,11... | collective-permute-start | bytes 147464 | tf_op jit(solution)/shard_map/ppermute | solution.py:172
  166.0 28.2 %collective-permute-start.1 = (bf16[6144,96]{0,1:T(8,128)(2,1)}, bf16[6144,96]{0,1:T(8,128)(2,1)}, u32[]{:S(2)}, u32[]{:S(2)}) collective-permute-start(bf16[6144,96]{0,1:T(8,128)(2,1)} %param.20), channel_id=1, source_target_pairs={{0,1},{1,0},{2,3},{3,2},{4,5},{5,4},{6,7},{7,6},{8,9},{9,8},{10,11... | collective-permute-start | bytes 3538952 | tf_op jit(solution)/shard_map/ppermute | solution.py:168
Sparse Core Ops, SparseCore 0:
  20.6 95.0 all-gather.3
  166.2 84.4 all-gather.5

commit v6 on v5

--- a/solution.py
+++ b/solution.py
@@ -172,7 +172,9 @@
     got = lax.ppermute(theirs, "yl", partner)
     pair_heads = jnp.stack([mine, got], axis=1)
     pair_heads = jnp.where(side == 0, pair_heads, pair_heads[:, ::-1])
-    every = lax.all_gather(pair_heads, ("x", "z"), axis=0, tiled=False)
+    along_z = lax.all_gather(pair_heads, "z", axis=0, tiled=False)
+    every = lax.all_gather(along_z, "x", axis=0, tiled=False)
+    every = every.reshape((-1,) + pair_heads.shape)
     pairs = every.shape[0]
     w_pair = jnp.stack([w_dense, other_w]).reshape(2, pairs, 2, head, width)
     mixed = lax.dot_general(

time: 286 us -> 283 us (0.990)
  waiting for transfers between devices: 157 us -> 123 us
  blocking collectives: 24.7 us -> 55.4 us
    all_gather x1, waiting for transfers between devices: 53.9 us -> 25.1 us  [dense_in_pairs(): every = lax.all_gather(along_z, 'x', axis=0, tiled=False)]
    all_gather x0 -> x1, blocking collectives: none -> 26.8 us  [dense_in_pairs(): along_z = lax.all_gather(pair_heads, 'z', axis=0, tiled=False)]
    ppermute x1, waiting for transfers between devices: 22.4 us -> 17 us  [dense_in_pairs(): other_w = lax.ppermute(w_dense, 'yl', partner)]
    all_to_all x1, blocking collectives: 15.5 us -> 19.5 us  [dense_in_pairs(): lax.all_to_all(ordered, ('x', 'z'), split_axis=0, concat_axis=2, tiled=True)]
  transfers between devices with their start and end apart: 4 -> 4, of which waited for: 4 -> 4; matrix products, arithmetic and copies ran while one was open for 8% -> 9% of each run, Pallas kernels for 0% -> 0%
where the time goes in v6:
time: 283 us; the launch traced here: 282 us
  waiting for transfers between devices  123 us (43%)
  blocking collectives  55.4 us (20%)
  local copies, waits for them, and re-layouts  43.8 us (15%)
  other arithmetic  27.8 us (10%)
  matrix products  13.5 us (5%)
  between operations  13.5 us (5%)
  starting transfers between devices  4.93 us (2%)
    all_gather x1, waiting for transfers between devices, gather_rows(): return lax.all_gather(pair, ('x', 'z'), axis=0, tiled=True)  76.4 us
    all_gather x1, blocking collectives, dense_in_pairs(): along_z = lax.all_gather(pair_heads, 'z', axis=0, tiled=False)  26.8 us
    all_gather x1, waiting for transfers between devices, dense_in_pairs(): every = lax.all_gather(along_z, 'x', axis=0, tiled=False)  25.1 us
    all_to_all x1, blocking collectives, dense_in_pairs(): lax.all_to_all(ordered, ('x', 'z'), split_axis=0, concat_axis=2, tiled=True)  19.5 us
    ppermute x1, waiting for transfers between devices, dense_in_pairs(): other_w = lax.ppermute(w_dense, 'yl', partner)  17 us
    all_gather x1, blocking collectives, gather_rows(): pair = lax.all_gather(block, 'yl', axis=0, tiled=True)  9.15 us
    unnamed x11, local copies, waits for them, and re-layouts  6.17 us
  transfers between devices with their start and end apart: 4, of which 4 were waited for; matrix products, arithmetic and copies ran while one was open for 9% of the time, Pallas kernels for 0%

profile of v6, /device:TPU:8, one launch (start us, length us, event | category | flops | bytes accessed | tf_op | source)
XLA Modules:
  0.0 281.7 jit_solution(3509901476321466404)
XLA Ops:
  11.3 9.1 %all_gather.18 = bf16[16,6144]{1,0:T(8,128)(2,1)} all-gather(bf16[8,6144]{1,0:T(8,128)(2,1)S(1)} %fusion.28), channel_id=1, replica_groups=mesh['rep'=8,'x'=4,'z'=8,'yl'=2] {'yl'}, dimensions={0}, use_global_device_ids=true | all-gather | bytes 294912 | tf_op jit(solution)/shard_map/all_gather | solution.py:109
  25.2 1.6 slice_bitcast_fusion.1
  26.8 2.1 gather_fusion.2
  28.9 2.1 gather_fusion.1
  36.0 1.6 slice_bitcast_fusion
  37.6 1.7 broadcast_select_fusion
  39.3 76.4 %all-gather.5.cloned.1.call-done = bf16[512,6144]{1,0:T(8,128)(2,1)} async-done(((bf16[16,6144]{1,0:T(8,128)(2,1)}), bf16[512,6144]{1,0:T(8,128)(2,1)}) %all-gather.5.cloned.1.call-update) | async-done | bytes 6291472 | tf_op jit(solution)/shard_map/all_gather | solution.py:110
  115.7 4.8 %fusion.69 = (bf16[512,288]{0,1:T(8,128)(2,1)S(1)}, f32[512,288]{0,1:T(8,128)S(1)}) fusion(f32[288]{0:T(512)} %convert_element_type.75, bf16[512,6144]{1,0:T(8,128)(2,1)} %all-gather.5.cloned.1.call-done, bf16[6144,288]{0,1:T(8,128)(2,1)S(1)} %copy-done), kind=kOutput, calls=%fused_computation.114 | convolution fusion | flops 1812234240 | bytes 10716288 | tf_op jit(solution)/shard_map/dot_general | solution.py:135
  124.9 1.6 reshape.213
  126.6 1.5 copy.44
  128.1 1.6 reshape.211
  129.7 1.6 reshape.212
  131.4 1.5 copy.42
  140.8 1.7 multiply_reduce_fusion
  147.1 2.9 %convolution_convert_fusion = bf16[4,120,96]{1,2,0:T(8,128)(2,1)} fusion(f32[4,120]{1,0:T(4,128)S(1)} %fusion.70, bf16[4,120,96]{1,2,0:T(8,128)(2,1)} %copy.44, bf16[4,128,96]{1,2,0:T(8,128)(2,1)} %get-tuple-element.22, f32[4,120,248]{2,1,0:T(8,128)} %copy-done.1, pred[120,248]{1,0:T(8,128)(4,1)} %iota_compare_fusion, ...), kind=kOutput, calls=%fused_computation.17 | convolution fusion | flops 24116696 | bytes 791704 | tf_op jit(solution)/shard_map/lsw,lwe->lse/dot_general | solution.py:43
  150.0 1.6 copy.45
  151.5 1.7 reshape.214
  153.2 1.6 pad_maximum_fusion.3
  154.8 1.6 copy.47
  158.0 2.4 collective-permute-start
  160.4 4.0 %collective-permute-done = bf16[32,8,96]{2,1,0:T(8,128)(2,1)} collective-permute-done((bf16[32,8,96]{2,1,0:T(8,128)(2,1)}, bf16[32,8,96]{2,1,0:T(8,128)(2,1)}, u32[]{:S(2)}, u32[]{:S(2)}) %collective-permute-start) | collective-permute-done | bytes 49184 | tf_op jit(solution)/shard_map/ppermute | solution.py:172
  165.4 26.8 %all-gather = bf16[256,2,8,96]{3,2,1,0:T(8,128)(2,1)S(1)} all-gather(bf16[32,2,8,96]{3,2,1,0:T(8,128)(2,1)S(1)} %reverse_select_fusion.1), channel_id=2, replica_groups=mesh['rep'=8,'x'=4,'z'=8,'yl'=2] {'z'}, dimensions={0}, use_global_device_ids=true | all-gather | bytes 884736 | tf_op jit(solution)/shard_map/all_gather | solution.py:175
  193.5 2.4 collective-permute-start.1
  196.0 2.5 copy.49
  199.4 17.0 %collective-permute-done.1 = bf16[6144,96]{0,1:T(8,128)(2,1)} collective-permute-done((bf16[6144,96]{0,1:T(8,128)(2,1)}, bf16[6144,96]{0,1:T(8,128)(2,1)}, u32[]{:S(2)}, u32[]{:S(2)}) %collective-permute-start.1) | collective-permute-done | bytes 1179680 | tf_op jit(solution)/shard_map/ppermute | solution.py:168
  216.4 2.6 copy.50
  218.9 25.1 %all-gather.7.cloned.1.call-done = bf16[32,32,2,8,96]{4,1,2,0,3:T(8,128)(2,1)} async-done(((bf16[8,32,2,8,96]{4,1,2,0,3:T(8,128)(2,1)}), bf16[32,32,2,8,96]{4,1,2,0,3:T(8,128)(2,1)}) %all-gather.7.cloned.1.call-update) | async-done | bytes 3145744 | tf_op jit(solution)/shard_map/all_gather | solution.py:176
  244.0 4.6 %fusion.14 = bf16[32,8,2,96]{3,0,2,1:T(8,128)(2,1)S(1)} fusion(bf16[1,32,2,96,96]{4,3,2,1,0:T(8,128)(2,1)} %bitcast.73, bf16[1,32,2,96,96]{4,3,2,1,0:T(8,128)(2,1)} %bitcast.72, bf16[32,32,2,8,96]{4,1,2,0,3:T(8,128)(2,1)} %all-gather.7.cloned.1.call-done, f32[2,96]{1,0:T(2,128)S(1)} %maximum_convert_fusion.1), kind=kOutput, calls=%fused_computation.16 | convolution fusion | flops 608796672 | bytes 5604096 | tf_op jit(solution)/shard_map/dot_general | solution.py:180
  249.4 1.7 reshape.218
  251.1 19.5 %all_to_all.4 = bf16[32,8,1,192]{3,1,2,0:T(8,128)(2,1)S(1)} all-to-all(bf16[32,8,1,192]{3,1,2,0:T(8,128)(2,1)} %bitcast.75), channel_id=1, replica_groups=mesh['rep'=8,'x'=4,'z'=8,'yl'=2] {'x','z'}, dimensions={0} | all-to-all | bytes 196608 | tf_op jit(solution)/shard_map/all_to_all | solution.py:191
  271.4 1.8 reshape.219
  273.2 1.6 fusion.29
  (64 shorter events, 37.5 us)
Async XLA Ops:
  6.5 109.2 %copy-start = (bf16[6144,288]{0,1:T(8,128)(2,1)S(1)}, bf16[6144,288]{0,1:T(8,128)(2,1)}, u32[]{:S(2)}) copy-start(bf16[6144,288]{0,1:T(8,128)(2,1)} %param.18) | copy-start | bytes 10616836
  6.5 109.2 %all-gather.5.cloned.1.call-start = ((), (), s32[]{:S(2)}) async-start(), calls=%async_computation.1 | async-start | bytes 6488064 | tf_op jit(solution)/shard_map/all_gather | solution.py:110
  20.5 223.6 %all-gather.7.cloned.1.call-start = ((), (), s32[]{:S(2)}) async-start(), calls=%async_computation.2 | async-start | bytes 5242880 | tf_op jit(solution)/shard_map/all_gather | solution.py:176
  24.4 0.6 copy-start.2
  39.3 82.6 %copy-start.3 = (f32[12]{0:T(128)S(1)}, f32[12]{0:T(128)}, u32[]{:S(2)}) copy-start(f32[12]{0:T(128)} %multiply_exponential_fusion) | copy-start | bytes 148
  145.2 0.8 copy-start.1
  158.0 6.5 %collective-permute-start = (bf16[32,8,96]{2,1,0:T(8,128)(2,1)}, bf16[32,8,96]{2,1,0:T(8,128)(2,1)}, u32[]{:S(2)}, u32[]{:S(2)}) collective-permute-start(bf16[32,8,96]{2,1,0:T(8,128)(2,1)} %get-tuple-element.19), channel_id=1, source_target_pairs={{0,1},{1,0},{2,3},{3,2},{4,5},{5,4},{6,7},{7,6},{8,9},{9,8},{10,11... | collective-permute-start | bytes 147464 | tf_op jit(solution)/shard_map/ppermute | solution.py:172
  193.5 22.9 %collective-permute-start.1 = (bf16[6144,96]{0,1:T(8,128)(2,1)}, bf16[6144,96]{0,1:T(8,128)(2,1)}, u32[]{:S(2)}, u32[]{:S(2)}) collective-permute-start(bf16[6144,96]{0,1:T(8,128)(2,1)} %param.20), channel_id=1, source_target_pairs={{0,1},{1,0},{2,3},{3,2},{4,5},{5,4},{6,7},{7,6},{8,9},{9,8},{10,11... | collective-permute-start | bytes 3538952 | tf_op jit(solution)/shard_map/ppermute | solution.py:168
Sparse Core Ops, SparseCore 0:
  20.6 95.0 all-gather.4
  193.6 50.3 all-gather.6

commit v7 on v4

--- a/solution.py
+++ b/solution.py
@@ -181,8 +181,9 @@
     own_first = jnp.stack([bias[side], bias[1 - side]]).astype(jnp.float32)
     attn = (mixed + own_first).astype(jnp.bfloat16)
     ordered = jnp.where(side == 0, attn, attn[:, :, ::-1])
-    own_rows = lax.all_to_all(ordered, ("x", "z"), split_axis=0, concat_axis=0, tiled=True)
-    return jnp.transpose(own_rows.reshape(pairs, per_device, 2 * width), (1, 0, 2)).reshape(per_device, -1)
+    ordered = ordered.reshape(pairs, per_device, 1, 2 * width)
+    own_rows = lax.all_to_all(ordered, ("x", "z"), split_axis=0, concat_axis=2, tiled=True)
+    return own_rows.reshape(per_device, -1)
 
 
 def solution(mesh):

time: 284 us -> 283 us (level)
  no operation moved by 1% of the time
where the time goes in v7:
time: 283 us; the launch traced here: 282 us
  waiting for transfers between devices  123 us (43%)
  blocking collectives  55.4 us (20%)
  local copies, waits for them, and re-layouts  43.8 us (15%)
  other arithmetic  27.8 us (10%)
  matrix products  13.5 us (5%)
  between operations  13.5 us (5%)
  starting transfers between devices  4.93 us (2%)
    all_gather x1, waiting for transfers between devices, gather_rows(): return lax.all_gather(pair, ('x', 'z'), axis=0, tiled=True)  76.4 us
    all_gather x1, blocking collectives, dense_in_pairs(): along_z = lax.all_gather(pair_heads, 'z', axis=0, tiled=False)  26.8 us
    all_gather x1, waiting for transfers between devices, dense_in_pairs(): every = lax.all_gather(along_z, 'x', axis=0, tiled=False)  25.1 us
    all_to_all x1, blocking collectives, dense_in_pairs(): lax.all_to_all(ordered, ('x', 'z'), split_axis=0, concat_axis=2, tiled=True)  19.5 us
    ppermute x1, waiting for transfers between devices, layer(): other_w = lax.ppermute(w_dense, 'yl', [(0, 1), (1, 0)])  17 us
    all_gather x1, blocking collectives, gather_rows(): pair = lax.all_gather(block, 'yl', axis=0, tiled=True)  9.15 us
    unnamed x11, local copies, waits for them, and re-layouts  6.17 us
  transfers between devices with their start and end apart: 4, of which 4 were waited for; matrix products, arithmetic and copies ran while one was open for 9% of the time, Pallas kernels for 0%

profile of v7, /device:TPU:8, one launch (start us, length us, event | category | flops | bytes accessed | tf_op | source)
XLA Modules:
  0.0 281.7 jit_solution(3509901476321466404)
XLA Ops:
  11.3 9.1 %all_gather.18 = bf16[16,6144]{1,0:T(8,128)(2,1)} all-gather(bf16[8,6144]{1,0:T(8,128)(2,1)S(1)} %fusion.28), channel_id=1, replica_groups=mesh['rep'=8,'x'=4,'z'=8,'yl'=2] {'yl'}, dimensions={0}, use_global_device_ids=true | all-gather | bytes 294912 | tf_op jit(solution)/shard_map/all_gather | solution.py:109
  25.2 1.6 slice_bitcast_fusion.1
  26.8 2.1 gather_fusion.2
  28.9 2.1 gather_fusion.1
  36.0 1.6 slice_bitcast_fusion
  37.6 1.7 broadcast_select_fusion
  39.3 76.4 %all-gather.5.cloned.1.call-done = bf16[512,6144]{1,0:T(8,128)(2,1)} async-done(((bf16[16,6144]{1,0:T(8,128)(2,1)}), bf16[512,6144]{1,0:T(8,128)(2,1)}) %all-gather.5.cloned.1.call-update) | async-done | bytes 6291472 | tf_op jit(solution)/shard_map/all_gather | solution.py:110
  115.7 4.8 %fusion.69 = (bf16[512,288]{0,1:T(8,128)(2,1)S(1)}, f32[512,288]{0,1:T(8,128)S(1)}) fusion(f32[288]{0:T(512)} %convert_element_type.75, bf16[512,6144]{1,0:T(8,128)(2,1)} %all-gather.5.cloned.1.call-done, bf16[6144,288]{0,1:T(8,128)(2,1)S(1)} %copy-done), kind=kOutput, calls=%fused_computation.114 | convolution fusion | flops 1812234240 | bytes 10716288 | tf_op jit(solution)/shard_map/dot_general | solution.py:130
  124.9 1.6 reshape.213
  126.6 1.5 copy.44
  128.1 1.6 reshape.211
  129.7 1.6 reshape.212
  131.4 1.5 copy.42
  140.8 1.7 multiply_reduce_fusion
  147.1 2.9 %convolution_convert_fusion = bf16[4,120,96]{1,2,0:T(8,128)(2,1)} fusion(f32[4,120]{1,0:T(4,128)S(1)} %fusion.70, bf16[4,120,96]{1,2,0:T(8,128)(2,1)} %copy.44, bf16[4,128,96]{1,2,0:T(8,128)(2,1)} %get-tuple-element.22, f32[4,120,248]{2,1,0:T(8,128)} %copy-done.1, pred[120,248]{1,0:T(8,128)(4,1)} %iota_compare_fusion, ...), kind=kOutput, calls=%fused_computation.17 | convolution fusion | flops 24116696 | bytes 791704 | tf_op jit(solution)/shard_map/lsw,lwe->lse/dot_general | solution.py:43
  150.0 1.6 copy.45
  151.5 1.7 reshape.214
  153.2 1.6 pad_maximum_fusion.3
  154.8 1.6 copy.47
  158.0 2.4 collective-permute-start
  160.4 4.0 %collective-permute-done = bf16[32,8,96]{2,1,0:T(8,128)(2,1)} collective-permute-done((bf16[32,8,96]{2,1,0:T(8,128)(2,1)}, bf16[32,8,96]{2,1,0:T(8,128)(2,1)}, u32[]{:S(2)}, u32[]{:S(2)}) %collective-permute-start) | collective-permute-done | bytes 49184 | tf_op jit(solution)/shard_map/ppermute | solution.py:166
  165.4 26.8 %all-gather = bf16[256,2,8,96]{3,2,1,0:T(8,128)(2,1)S(1)} all-gather(bf16[32,2,8,96]{3,2,1,0:T(8,128)(2,1)S(1)} %reverse_select_fusion.1), channel_id=2, replica_groups=mesh['rep'=8,'x'=4,'z'=8,'yl'=2] {'z'}, dimensions={0}, use_global_device_ids=true | all-gather | bytes 884736 | tf_op jit(solution)/shard_map/all_gather | solution.py:169
  193.5 2.4 collective-permute-start.1
  196.0 2.5 copy.49
  199.4 17.0 %collective-permute-done.1 = bf16[6144,96]{0,1:T(8,128)(2,1)} collective-permute-done((bf16[6144,96]{0,1:T(8,128)(2,1)}, bf16[6144,96]{0,1:T(8,128)(2,1)}, u32[]{:S(2)}, u32[]{:S(2)}) %collective-permute-start.1) | collective-permute-done | bytes 1179680 | tf_op jit(solution)/shard_map/ppermute | solution.py:128
  216.4 2.6 copy.50
  218.9 25.1 %all-gather.7.cloned.1.call-done = bf16[32,32,2,8,96]{4,1,2,0,3:T(8,128)(2,1)} async-done(((bf16[8,32,2,8,96]{4,1,2,0,3:T(8,128)(2,1)}), bf16[32,32,2,8,96]{4,1,2,0,3:T(8,128)(2,1)}) %all-gather.7.cloned.1.call-update) | async-done | bytes 3145744 | tf_op jit(solution)/shard_map/all_gather | solution.py:170
  244.0 4.6 %fusion.14 = bf16[32,8,2,96]{3,0,2,1:T(8,128)(2,1)S(1)} fusion(bf16[1,32,2,96,96]{4,3,2,1,0:T(8,128)(2,1)} %bitcast.73, bf16[1,32,2,96,96]{4,3,2,1,0:T(8,128)(2,1)} %bitcast.72, bf16[32,32,2,8,96]{4,1,2,0,3:T(8,128)(2,1)} %all-gather.7.cloned.1.call-done, f32[2,96]{1,0:T(2,128)S(1)} %maximum_convert_fusion.1), kind=kOutput, calls=%fused_computation.16 | convolution fusion | flops 608796672 | bytes 5604096 | tf_op jit(solution)/shard_map/dot_general | solution.py:174
  249.4 1.7 reshape.218
  251.1 19.5 %all_to_all.4 = bf16[32,8,1,192]{3,1,2,0:T(8,128)(2,1)S(1)} all-to-all(bf16[32,8,1,192]{3,1,2,0:T(8,128)(2,1)} %bitcast.75), channel_id=1, replica_groups=mesh['rep'=8,'x'=4,'z'=8,'yl'=2] {'x','z'}, dimensions={0} | all-to-all | bytes 196608 | tf_op jit(solution)/shard_map/all_to_all | solution.py:185
  271.4 1.8 reshape.219
  273.2 1.6 fusion.29
  (64 shorter events, 37.5 us)
Async XLA Ops:
  6.5 109.2 %copy-start = (bf16[6144,288]{0,1:T(8,128)(2,1)S(1)}, bf16[6144,288]{0,1:T(8,128)(2,1)}, u32[]{:S(2)}) copy-start(bf16[6144,288]{0,1:T(8,128)(2,1)} %param.18) | copy-start | bytes 10616836
  6.5 109.2 %all-gather.5.cloned.1.call-start = ((), (), s32[]{:S(2)}) async-start(), calls=%async_computation.1 | async-start | bytes 6488064 | tf_op jit(solution)/shard_map/all_gather | solution.py:110
  20.5 223.6 %all-gather.7.cloned.1.call-start = ((), (), s32[]{:S(2)}) async-start(), calls=%async_computation.2 | async-start | bytes 5242880 | tf_op jit(solution)/shard_map/all_gather | solution.py:170
  24.4 0.6 copy-start.2
  39.3 82.6 %copy-start.3 = (f32[12]{0:T(128)S(1)}, f32[12]{0:T(128)}, u32[]{:S(2)}) copy-start(f32[12]{0:T(128)} %multiply_exponential_fusion) | copy-start | bytes 148
  145.2 0.8 copy-start.1
  158.0 6.5 %collective-permute-start = (bf16[32,8,96]{2,1,0:T(8,128)(2,1)}, bf16[32,8,96]{2,1,0:T(8,128)(2,1)}, u32[]{:S(2)}, u32[]{:S(2)}) collective-permute-start(bf16[32,8,96]{2,1,0:T(8,128)(2,1)} %get-tuple-element.19), channel_id=1, source_target_pairs={{0,1},{1,0},{2,3},{3,2},{4,5},{5,4},{6,7},{7,6},{8,9},{9,8},{10,11... | collective-permute-start | bytes 147464 | tf_op jit(solution)/shard_map/ppermute | solution.py:166
  193.5 22.9 %collective-permute-start.1 = (bf16[6144,96]{0,1:T(8,128)(2,1)}, bf16[6144,96]{0,1:T(8,128)(2,1)}, u32[]{:S(2)}, u32[]{:S(2)}) collective-permute-start(bf16[6144,96]{0,1:T(8,128)(2,1)} %param.20), channel_id=1, source_target_pairs={{0,1},{1,0},{2,3},{3,2},{4,5},{5,4},{6,7},{7,6},{8,9},{9,8},{10,11... | collective-permute-start | bytes 3538952 | tf_op jit(solution)/shard_map/ppermute | solution.py:128
Sparse Core Ops, SparseCore 0:
  20.6 95.0 all-gather.4
  193.6 50.3 all-gather.6
